TPU v7x, 256 devices: a whole 4x4x8 slice. The times are simulated.
256 devices in a mesh: ang: 128 (over z, x_lo, y, core), sl: 2 (over x_hi).
Axes of the slice: x: 4 (x_hi: 2, x_lo: 2; x = x_hi * 2 + x_lo), y: 4, z: 8, core: 2. Of those that a mesh axis runs over, the one named last changes fastest.
Arguments:
- projections: float32 [256, 8, 4352], P('ang', 'sl'), may hold values from -6 to 6
- partner: int32 [256], replicated, may hold values from 0 to 255, as said below
- offsets: int32 [256], P('ang'), may hold values from 0 to 192
- angles: float32 [256], replicated, may hold values from 0 to 6.2832, as said below
- coefficients: float32 [2, 8, 4096, 1280], P(None, None, ('ang', 'sl')), may hold values from -6 to 6
Outputs:
- updated: float32 [2, 8, 4096, 1280], P(None, None, ('ang', 'sl'))
- misfit: float32 [256, 8], P('ang', 'sl')
Inputs may be any that keep to these rules, and one draw needn't show every extreme that they name: partner[partner[g]] = g, and g // 2 and partner[g] // 2 differ by 64: a projection's partner lies on the index of ang half the axis away. angles[partner[g]] lies within pi / 128 of angles[g] + pi or angles[g] - pi.
All inputs are finite; a program needn't handle non-finite values.
Results may differ from a plain program's by a relative error of at most 0.0003.
Values sent between devices are 32-bit elements; how exact they have to be, the bound alone decides.
No kernel may reach another device: no remote copies, remote signals or barrier semaphores. Data moves between devices by JAX's collectives and lax.ppermute only.
A program may use at most 64 MiB of HBM per device.

v0:
```python
import math

import jax
import jax.numpy as jnp
from jax import lax
from jax.sharding import Mesh
from jax.sharding import PartitionSpec as P


W = 8192
HALF = 4096
K = 4096
EXTRA = 256
RAMP = 64
ROWS = 8
ANG = ("ang_0", "ang_1", "ang_2", "ang_3")
ANG_SL = ("ang_0", "ang_1", "ang_2", "ang_3", "sl")


paganin_strength = 16.0
small_eps = 1e-06
highest = lax.Precision.HIGHEST


def from_behind(value, axis, steps):
    count = lax.axis_size(axis)
    pairs = [(source, (source + steps) % count) for source in range(count)]
    return lax.ppermute(value, axis, pairs)


def paganin_rows(frequencies):
    row_ids = jnp.arange(ROWS, dtype=jnp.int32)
    row_offset = (row_ids[:, None] - row_ids[None, :]) % ROWS
    cos_table = jnp.cos(
        2.0
        * math.pi
        / ROWS
        * (row_ids[:, None, None] * row_offset[None, :, :] % ROWS).astype(jnp.float32)
    )
    row_freq = jnp.minimum(row_ids, ROWS - row_ids).astype(jnp.float32) / ROWS
    col_freq = frequencies / W
    damping = 1.0 / (
        1.0
        + paganin_strength
        * (col_freq[:, None] * col_freq[:, None] + row_freq[None, :] * row_freq[None, :])
    )
    return jnp.einsum("nq,qij->nij", damping, cos_table, precision=highest) / ROWS


def blend_band(projections, mirrored, offsets):
    position = jnp.arange(EXTRA, dtype=jnp.int32).astype(jnp.float32)
    weight = jnp.clip((position[None, :] - offsets[:, None].astype(jnp.float32)) / RAMP, 0.0, 1.0)
    own_band = projections[:, :, HALF - EXTRA : HALF]
    blended = own_band + weight[:, None, :] * (mirrored - own_band)
    return jnp.concatenate([projections[:, :, : HALF - EXTRA], blended], axis=2)


def spectrum_of(stitched):
    row_count = stitched.shape[0] * stitched.shape[1]
    low_split = W // 128
    outer_count = HALF // low_split
    high_count = K // 128
    folded = stitched.reshape(row_count, outer_count, low_split)
    norm_scale = 1.0 / math.sqrt(HALF)
    outer_ids = jnp.arange(outer_count, dtype=jnp.int32)
    lane_ids = jnp.arange(128, dtype=jnp.int32)
    first_phase = (
        2.0 * math.pi / 128 * (outer_ids[:, None] * lane_ids[None, :] % 128).astype(jnp.float32)
    )
    first_cos = jnp.cos(first_phase) * norm_scale
    first_sin = jnp.sin(first_phase) * norm_scale
    part_real = jnp.einsum("rab,ap->rbp", folded, first_cos, precision=highest)
    part_imag = -jnp.einsum("rab,ap->rbp", folded, first_sin, precision=highest)
    low_ids = jnp.arange(low_split, dtype=jnp.int32)
    twist_phase = 2.0 * math.pi / W * (low_ids[:, None] * lane_ids[None, :]).astype(jnp.float32)
    twist_cos = jnp.cos(twist_phase)
    twist_sin = jnp.sin(twist_phase)
    turned_real = part_real * twist_cos + part_imag * twist_sin
    turned_imag = part_imag * twist_cos - part_real * twist_sin
    high_ids = jnp.arange(high_count, dtype=jnp.int32)
    last_phase = (
        2.0
        * math.pi
        / low_split
        * (low_ids[:, None] * high_ids[None, :] % low_split).astype(jnp.float32)
    )
    last_cos = jnp.cos(last_phase)
    last_sin = jnp.sin(last_phase)
    spec_real = jnp.einsum("rbp,bq->rqp", turned_real, last_cos, precision=highest) + jnp.einsum(
        "rbp,bq->rqp", turned_imag, last_sin, precision=highest
    )
    spec_imag = jnp.einsum("rbp,bq->rqp", turned_imag, last_cos, precision=highest) - jnp.einsum(
        "rbp,bq->rqp", turned_real, last_sin, precision=highest
    )
    return (spec_real, spec_imag)


def step_body(projections, partner, offsets, angles, coefficients):
    ang_count = lax.axis_size(ANG)
    sl_count = lax.axis_size("sl")
    ang_index = lax.axis_index(ANG)
    sl_index = lax.axis_index("sl")
    per_dev = projections.shape[0]
    rows_dev = projections.shape[1]
    total_angles = per_dev * ang_count
    block_freqs = coefficients.shape[2]
    harmonics = coefficients.shape[3]
    columns = ROWS * block_freqs
    own_partners = lax.dynamic_slice_in_dim(partner, ang_index * per_dev, per_dev)
    across_dev = (ang_index + ang_count // 2) % ang_count
    partner_slots = own_partners - across_dev * per_dev
    arrived = from_behind(projections[:, :, HALF:], ANG, ang_count // 2)
    mirrored = jnp.flip(jnp.take(arrived, partner_slots, axis=0), axis=2)
    stitched = blend_band(projections, mirrored, offsets)
    spec_real, spec_imag = spectrum_of(stitched)
    spectra = jnp.stack([spec_real, spec_imag])
    dev_count = ang_count * sl_count
    lane_split = 128 // block_freqs
    spectra = spectra.reshape(2, per_dev * rows_dev, K // 128, lane_split, block_freqs)
    payload = spectra.transpose(2, 3, 0, 1, 4).reshape(dev_count, -1)
    received = lax.all_to_all(payload, ANG_SL, 0, 0, tiled=True)
    received = received.reshape(ang_count, sl_count, 2, per_dev, rows_dev * block_freqs)
    freq_major = received.transpose(2, 0, 3, 1, 4).reshape(2, total_angles, columns)
    freq_base = (ang_index * sl_count + sl_index) * block_freqs
    local_freq = (freq_base + jnp.arange(block_freqs, dtype=jnp.int32)).astype(jnp.float32)
    col_freq = jnp.tile(local_freq, ROWS)
    turn_phase = 2.0 * math.pi / W * col_freq
    turn_cos = jnp.cos(turn_phase)
    turn_sin = jnp.sin(turn_phase)
    own_real = freq_major[0]
    own_imag = freq_major[1]
    swap = (partner[:, None] == jnp.arange(total_angles, dtype=jnp.int32)[None, :]).astype(jnp.float32)
    own_both = jnp.concatenate([own_real, own_imag], axis=1)
    pair_both = jnp.dot(swap, own_both, precision=highest)
    pair_real = pair_both[:, :columns]
    pair_imag = pair_both[:, columns:]
    comb_real = own_real + turn_cos * pair_real + turn_sin * pair_imag
    comb_imag = own_imag + turn_sin * pair_real - turn_cos * pair_imag
    rows_matrix = paganin_rows(local_freq)
    full_matrix = jnp.einsum(
        "nij,mn->jmin", rows_matrix, jnp.eye(block_freqs, dtype=jnp.float32)
    ).reshape(columns, columns)
    filt_real = jnp.dot(comb_real, full_matrix, precision=highest)
    filt_imag = jnp.dot(comb_imag, full_matrix, precision=highest)
    ramp_weights = (col_freq + 0.5) / K
    coef_rows = coefficients.reshape(2 * columns, harmonics)
    harm_shift = (jnp.arange(harmonics, dtype=jnp.int32) - harmonics // 2).astype(jnp.float32)
    norm_scale = 1.0 / math.sqrt(harmonics)
    phase_tab = angles[:, None] * harm_shift[None, :]
    tabs = jnp.concatenate(
        [jnp.cos(phase_tab) * norm_scale, jnp.sin(phase_tab) * norm_scale]
    )

    def to_image(coef):
        prod = lax.dot_general(
            tabs, coef, (((1,), (1,)), ((), ())), precision=highest
        )
        cos_part, sin_part = prod[:total_angles], prod[total_angles:]
        real = cos_part[:, :columns] - sin_part[:, columns:]
        imag = cos_part[:, columns:] + sin_part[:, :columns]
        return real, imag

    model_real, model_imag = to_image(coef_rows)
    diff_real = model_real - filt_real
    diff_imag = model_imag - filt_imag
    resid_real = ramp_weights * diff_real
    resid_imag = ramp_weights * diff_imag
    energy = (diff_real * resid_real + diff_imag * resid_imag).reshape(
        total_angles, ROWS, block_freqs
    )
    misfit_table = jnp.sum(energy, axis=2) / K
    stacked = jnp.concatenate(
        [
            jnp.concatenate([resid_real, resid_imag], axis=1),
            jnp.concatenate([resid_imag, -resid_real], axis=1),
        ]
    )
    gram = lax.dot_general(tabs, tabs, (((1,), (1,)), ((), ())), precision=highest)
    gram_real = gram[:total_angles, :total_angles] + gram[total_angles:, total_angles:]
    gram_imag = gram[total_angles:, :total_angles] - gram[:total_angles, total_angles:]
    gram_both = jnp.concatenate(
        [
            jnp.concatenate([gram_real, -gram_imag], axis=1),
            jnp.concatenate([gram_imag, gram_real], axis=1),
        ]
    )
    resid_both = jnp.concatenate([resid_real, resid_imag])
    image_both = jnp.dot(gram_both, resid_both, precision=highest)
    image_real, image_imag = image_both[:total_angles], image_both[total_angles:]
    curvature = jnp.sum(ramp_weights * (image_real * image_real + image_imag * image_imag))
    grad_norm = jnp.sum(resid_real * image_real + resid_imag * image_imag)
    by_owner = misfit_table.reshape(ang_count, per_dev, sl_count, rows_dev)
    by_owner = jnp.swapaxes(by_owner, 1, 2).reshape(ang_count * sl_count, per_dev * rows_dev)
    scalars = jnp.broadcast_to(jnp.stack([grad_norm, curvature])[None], (ang_count * sl_count, 2))
    payload = jnp.concatenate([by_owner, scalars], axis=1)
    received = lax.all_to_all(payload, ANG_SL, 0, 0, tiled=True)
    totals = jnp.sum(received, axis=0)
    misfit = totals[: per_dev * rows_dev].reshape(per_dev, rows_dev)
    step_size = totals[per_dev * rows_dev] / (totals[per_dev * rows_dev + 1] + small_eps)
    grad = lax.dot_general(stacked, tabs, (((0,), (0,)), ((), ())), precision=highest)
    updated = coefficients - step_size * grad.reshape(coefficients.shape)
    return (updated, misfit)


def solution(mesh):
    torus = Mesh(
        mesh.devices.reshape(8, 2, 4, 2, mesh.shape["sl"]),
        ("ang_0", "ang_1", "ang_2", "ang_3", "sl"),
    )
    in_specs = (P(ANG, "sl", None), P(), P(ANG), P(), P(None, None, ANG_SL, None))
    out_specs = (P(None, None, ANG_SL, None), P(ANG, "sl"))
    return jax.shard_map(
        step_body, mesh=torus, in_specs=in_specs, out_specs=out_specs, check_vma=False
    )
```

profile of v0, /device:TPU:1, one launch (start us, length us, event | category | flops | bytes accessed | tf_op | source)
XLA Modules:
  0.0 97.7 jit_solution(10949854827765617448)
XLA Ops:
  0.6 0.7 slice.72
  1.3 7.7 %collective-permute-start = (f32[2,4,256]{2,1,0:T(4,128)S(1)}, f32[2,4,256]{2,1,0:T(4,128)S(1)}, u32[]{:S(2)}, u32[]{:S(2)}) collective-permute-start(f32[2,4,256]{2,1,0:T(4,128)S(1)} %slice.72), channel_id=1, source_target_pairs={{0,128},{2,130},{4,132},{6,134},{8,136},{10,138},{12,140},{14,142}... | collective-permute-start | bytes 24584 | tf_op jit(solution)/shard_map/ppermute | solution.py:28
  10.4 0.9 multiply_bitcast_fusion
  11.2 5.4 %fusion.2 = (f32[256,1280]{1,0:T(8,128)S(1)}, f32[256,1280]{1,0:T(8,128)S(1)}) fusion(f32[1280]{0:T(1024)S(1)} %add_convert_fusion, f32[256]{0:T(256)} %param.8), kind=kLoop, calls=%fused_computation.7 | loop fusion | flops 983040 | bytes 2627584 | tf_op jit(solution)/shard_map/mul | solution.py:151
  16.6 5.3 %fusion = f32[512,512]{0,1:T(8,128)} fusion(f32[256,1280]{1,0:T(8,128)S(1)} %get-tuple-element.13, f32[256,1280]{1,0:T(8,128)S(1)} %get-tuple-element.12), kind=kOutput, calls=%fused_computation.5 | convolution fusion | flops 4027187200 | bytes 3670016 | tf_op jit(solution)/shard_map/dot_general | solution.py:178
  25.7 1.0 %copy.39 = f32[8,32,128]{1,2,0:T(8,128)} copy(f32[8,32,128]{2,1,0:T(8,128)S(1)} %fusion.5) | data formatting | bytes 262144 | tf_op jit(solution)/shard_map/add | solution.py:89
  27.3 2.1 %maximum_bitcast_fusion = f32[32,8,2,8,16]{0,4,1,3,2:T(8,128)} fusion(f32[1,8,32,8,16]{2,4,3,1,0:T(8,128)S(1)} %bitcast.61, f32[1,8,32,8,16]{2,4,3,1,0:T(8,128)} %bitcast.59), kind=kLoop, calls=%fused_computation.18 | loop fusion | flops 65536 | bytes 524288 | tf_op jit(solution)/shard_map/transpose | solution.py:120
  29.4 4.0 %copy.41 = f32[32,8,2,8,16]{4,3,2,1,0:T(8,128)} copy(f32[32,8,2,8,16]{0,4,1,3,2:T(8,128)} %maximum_bitcast_fusion) | data formatting | bytes 524288 | tf_op jit(solution)/shard_map/transpose | solution.py:120
  33.4 3.1 %all_to_all.16 = f32[256,1,256]{2,1,0:T(1,128)} reshape(f32[32,8,2,8,16]{4,3,2,1,0:T(8,128)} %copy.41) | data formatting | bytes 524288 | tf_op jit(solution)/shard_map/all_to_all | solution.py:121
  36.4 10.9 %all-to-all-start = ((f32[256,1,256]{2,1,0:T(1,128)}), f32[256,1,256]{2,1,0:T(1,128)}, u32[]{:S(2)}, u32[]{:S(2)}) async-start(f32[256,1,256]{2,1,0:T(1,128)} %all_to_all.16), calls=%async_computation | async-start | bytes 524288 | tf_op jit(solution)/shard_map/all_to_all | solution.py:121
  47.4 0.8 reshape.193
  48.4 2.2 %fusion.154 = (f32[256,256]{0,1:T(8,128)}, f32[256,256]{0,1:T(8,128)}, f32[256,256]{0,1:T(8,128)}) fusion(f32[512,512]{0,1:T(8,128)} %fusion), kind=kLoop, calls=%fused_computation.204 | loop fusion | flops 196608 | bytes 1835008 | tf_op jit(solution)/shard_map/neg | solution.py:183
  50.6 3.3 %fusion.1 = f32[512,256]{0,1:T(8,128)} fusion(f32[256,1280]{1,0:T(8,128)S(1)} %bitcast.58, f32[256,1280]{1,0:T(8,128)S(1)} %get-tuple-element.13, f32[256,1280]{1,0:T(8,128)S(1)} %get-tuple-element.12), kind=kOutput, calls=%fused_computation.6 | convolution fusion | flops 2013921280 | bytes 4456448 | tf_op jit(solution)/shard_map/dot_general | solution.py:155
  53.9 7.9 %all-to-all-done = f32[256,1,256]{2,1,0:T(1,128)} async-done(((f32[256,1,256]{2,1,0:T(1,128)}), f32[256,1,256]{2,1,0:T(1,128)}, u32[]{:S(2)}, u32[]{:S(2)}) %all-to-all-start) | async-done | bytes 262176 | tf_op jit(solution)/shard_map/all_to_all | solution.py:121
  61.8 1.6 %reduce.1 = f32[256,256]{1,0:T(8,128)S(1)} reduce(f32[256,1,256]{2,1,0:T(1,128)} %all-to-all-done, f32[]{:T(128)} %constant.146), dimensions={1}, to_apply=%all_to_all.13.reduce_sub_computation | reduce | bytes 524292 | tf_op jit(solution)/shard_map/all_to_all | solution.py:121
  63.7 0.9 fusion.155
  64.9 1.8 %copy.44 = f32[1,128,2,2,64]{4,3,2,1,0:T(2,128)} copy(f32[1,128,2,2,64]{4,2,0,3,1:T(2,128)} %get-tuple-element.10) | data formatting | bytes 262144 | tf_op jit(solution)/shard_map/slice | solution.py:131
  66.8 1.1 %squeeze.9 = f32[256,128]{1,0:T(8,128)S(1)} reshape(f32[1,128,2,2,64]{4,3,2,1,0:T(2,128)} %copy.44) | data formatting | bytes 262144 | tf_op jit(solution)/shard_map/squeeze | solution.py:131
  69.1 0.7 fusion.7
  69.8 0.7 add_reduce_fusion
  71.2 1.4 %pad_maximum_fusion.6 = f32[10]{0:T(128)S(1)} fusion(f32[1]{0:T(128)} %bitcast.18, f32[1]{0:T(128)} %bitcast.17), kind=kLoop, calls=%fused_computation.159 | loop fusion | flops 10 | bytes 48 | tf_op jit(solution)/shard_map/stack | solution.py:194
  72.6 18.8 %all_to_all.19 = f32[256,1,10]{2,1,0:T(1,128)S(1)} all-to-all(f32[256,1,10]{2,1,0:T(1,128)S(1)} %bitcast.63), channel_id=1, replica_groups=mesh['ang_0'=8,'ang_1'=2,'ang_2'=4,'ang_3'=2,'sl'=2] {'ang_0','ang_1','a..., dimensions={0} | all-to-all | bytes 20480 | tf_op jit(solution)/shard_map/all_to_all | solution.py:196
  93.5 2.3 %convolution_multiply_fusion = f32[256,1280]{1,0:T(8,128)S(1)} fusion(f32[256,1280]{1,0:T(8,128)S(1)} %get-tuple-element.13, f32[256,1280]{1,0:T(8,128)S(1)} %get-tuple-element.12, f32[]{:T(128)} %bitcast.21, f32[256,128]{0,1:T(8,128)S(1)} %get-tuple-element.11, f32[256,128]{0,1:T(8,128)S(1)} %get-tuple-element.17, f32[256,128]{0,1:T(8,128)S(1)} %get-tuple-element.16), kind=kOutput, calls=%fused_computation.1 | convolution fusion | flops 2014642176 | bytes 4325380 | tf_op jit(solution)/shard_map/dot_general | solution.py:200
  95.9 1.2 %sub.100 = f32[2,8,16,1280]{3,2,1,0:T(8,128)} subtract(f32[2,8,16,1280]{3,2,1,0:T(8,128)S(1)} %copy-done.1, f32[2,8,16,1280]{3,2,1,0:T(8,128)S(1)} %bitcast.57) | non-fusion elementwise | flops 327680 | bytes 3932160 | tf_op jit(solution)/shard_map/sub | solution.py:201
  (72 shorter events, 9.7 us)
Async XLA Ops:
  1.3 20.7 %collective-permute-start = (f32[2,4,256]{2,1,0:T(4,128)S(1)}, f32[2,4,256]{2,1,0:T(4,128)S(1)}, u32[]{:S(2)}, u32[]{:S(2)}) collective-permute-start(f32[2,4,256]{2,1,0:T(4,128)S(1)} %slice.72), channel_id=1, source_target_pairs={{0,128},{2,130},{4,132},{6,134},{8,136},{10,138},{12,140},{14,142}... | collective-permute-start | bytes 24584 | tf_op jit(solution)/shard_map/ppermute | solution.py:28
  16.6 5.3 %copy-start.9 = (s32[256]{0:T(256)S(1)}, s32[256]{0:T(256)}, u32[]{:S(2)}) copy-start(s32[256]{0:T(256)} %param.6) | copy-start | bytes 3076
  16.6 6.4 %copy-start.5 = (f32[2,4,4352]{2,1,0:T(4,128)S(1)}, f32[2,4,4352]{2,1,0:T(4,128)}, u32[]{:S(2)}) copy-start(f32[2,4,4352]{2,1,0:T(4,128)} %param.5) | copy-start | bytes 417796
  16.6 6.4 %slice-start = ((f32[2,4,4352]{2,1,0:T(4,128)}), f32[2,4,3840]{2,1,0:T(4,128)S(1)}, s32[]{:S(2)}) async-start(f32[2,4,4352]{2,1,0:T(4,128)} %param.5), calls=%async_computation.2 | async-start | bytes 245760 | tf_op jit(solution)/shard_map/slice | solution.py:55
  33.4 14.0 %copy-start.2 = (f32[8,16,8,16]{3,2,1,0:T(8,128)S(1)}, f32[8,16,8,16]{3,2,1,0:T(8,128)}, u32[]{:S(2)}) copy-start(f32[8,16,8,16]{3,2,1,0:T(8,128)} %multiply_bitcast_fusion) | copy-start | bytes 196612
  36.4 25.4 %all-to-all-start = ((f32[256,1,256]{2,1,0:T(1,128)}), f32[256,1,256]{2,1,0:T(1,128)}, u32[]{:S(2)}, u32[]{:S(2)}) async-start(f32[256,1,256]{2,1,0:T(1,128)} %all_to_all.16), calls=%async_computation | async-start | bytes 524288 | tf_op jit(solution)/shard_map/all_to_all | solution.py:121
  48.4 2.2 %copy-start = (f32[2,8,16,1280]{3,2,1,0:T(8,128)S(1)}, f32[2,8,16,1280]{3,2,1,0:T(8,128)}, u32[]{:S(2)}) copy-start(f32[2,8,16,1280]{3,2,1,0:T(8,128)} %param.9) | copy-start | bytes 3932164
  64.6 3.6 %copy-start.3 = (f32[512,256]{0,1:T(8,128)S(1)}, f32[512,256]{0,1:T(8,128)}, u32[]{:S(2)}) copy-start(f32[512,256]{0,1:T(8,128)} %fusion.1) | copy-start | bytes 1572868
  64.9 3.3 %copy-start.4 = (f32[128,128]{1,0:T(8,128)S(1)}, f32[128,128]{1,0:T(8,128)}, u32[]{:S(2)}) copy-start(f32[128,128]{1,0:T(8,128)} %reshape.193) | copy-start | bytes 196612
  67.9 1.1 %copy-start.6 = (f32[256,256]{0,1:T(8,128)S(1)}, f32[256,256]{0,1:T(8,128)}, u32[]{:S(2)}) copy-start(f32[256,256]{0,1:T(8,128)} %get-tuple-element.4) | copy-start | bytes 786436
  67.9 1.1 %copy-start.7 = (f32[256,256]{0,1:T(8,128)S(1)}, f32[256,256]{0,1:T(8,128)}, u32[]{:S(2)}) copy-start(f32[256,256]{0,1:T(8,128)} %get-tuple-element.5) | copy-start | bytes 786436
  67.9 1.2 %copy-start.8 = (f32[256,256]{0,1:T(8,128)S(1)}, f32[256,256]{0,1:T(8,128)}, u32[]{:S(2)}) copy-start(f32[256,256]{0,1:T(8,128)} %get-tuple-element.8) | copy-start | bytes 786436
  93.5 2.3 %copy-start.1 = (f32[2,8,16,1280]{3,2,1,0:T(8,128)S(1)}, f32[2,8,16,1280]{3,2,1,0:T(8,128)}, u32[]{:S(2)}) copy-start(f32[2,8,16,1280]{3,2,1,0:T(8,128)} %param.9) | copy-start | bytes 3932164
where the time goes:
time: 98.2 us; the launch traced here: 97.7 us
  blocking collectives  18.8 us (19%)
  starting transfers between devices  18.6 us (19%)
  local copies, waits for them, and re-layouts  17.5 us (18%)
  other arithmetic  16.9 us (17%)
  matrix products  15.7 us (16%)
  waiting for transfers between devices  7.94 us (8%)
  between operations  2.29 us (2%)
    all_to_all x1, blocking collectives, step_body(): received = lax.all_to_all(payload, ANG_SL, 0, 0, tiled=True)  18.8 us
    all_to_all x1, starting transfers between devices, step_body(): received = lax.all_to_all(payload, ANG_SL, 0, 0, tiled=True)  10.9 us
    all_to_all x1, waiting for transfers between devices, step_body(): received = lax.all_to_all(payload, ANG_SL, 0, 0, tiled=True)  7.93 us
    ppermute x1, starting transfers between devices, from_behind(): return lax.ppermute(value, axis, pairs)  7.73 us
    mul x1, other arithmetic, step_body(): jnp.cos(phase_tab) * norm_scale  5.36 us
    dot_general x1, matrix products, step_body(): lax.dot_general(tabs, tabs, (((1,), (1,)), ((), ())), precision=highest)  5.3 us
    transpose x1, local copies, waits for them, and re-layouts, step_body(): payload = spectra.transpose(2, 3, 0, 1, 4).reshape(dev_count, -1)  3.99 us
    dot_general x1, matrix products, to_image(): lax.dot_general(tabs, coef, (((1,), (1,)), ((), ())), precision=highest)  3.29 us
  transfers between devices with their start and end apart: 2, of which 1 were waited for; matrix products, arithmetic and copies ran while one was open for 20% of the time, Pallas kernels for 0%

commit v1 on v0

--- a/solution.py
+++ b/solution.py
@@ -119,18 +119,29 @@
     spectra = spectra.reshape(2, per_dev * rows_dev, K // 128, lane_split, block_freqs)
     payload = spectra.transpose(2, 3, 0, 1, 4).reshape(dev_count, -1)
     received = lax.all_to_all(payload, ANG_SL, 0, 0, tiled=True)
-    received = received.reshape(ang_count, sl_count, 2, per_dev, rows_dev * block_freqs)
-    freq_major = received.transpose(2, 0, 3, 1, 4).reshape(2, total_angles, columns)
+    if per_dev == 2 and sl_count == 2:
+        half = rows_dev * block_freqs
+        row_ids = jnp.arange(dev_count, dtype=jnp.int32)
+        lane_ids = jnp.arange(2 * columns, dtype=jnp.int32)
+        row_swap = ((row_ids[:, None] ^ 1) == row_ids[None, :]).astype(jnp.float32)
+        lane_swap = ((lane_ids[:, None] ^ half) == lane_ids[None, :]).astype(jnp.float32)
+        swapped = jnp.dot(
+            row_swap, jnp.dot(received, lane_swap, precision=highest), precision=highest
+        )
+        same_half = (row_ids[:, None] % 2) == ((lane_ids[None, :] // half) % 2)
+        own_both = jnp.where(same_half, received, swapped)
+    else:
+        received = received.reshape(ang_count, sl_count, 2, per_dev, rows_dev * block_freqs)
+        own_both = received.transpose(0, 3, 2, 1, 4).reshape(total_angles, 2 * columns)
     freq_base = (ang_index * sl_count + sl_index) * block_freqs
     local_freq = (freq_base + jnp.arange(block_freqs, dtype=jnp.int32)).astype(jnp.float32)
     col_freq = jnp.tile(local_freq, ROWS)
     turn_phase = 2.0 * math.pi / W * col_freq
     turn_cos = jnp.cos(turn_phase)
     turn_sin = jnp.sin(turn_phase)
-    own_real = freq_major[0]
-    own_imag = freq_major[1]
+    own_real = own_both[:, :columns]
+    own_imag = own_both[:, columns:]
     swap = (partner[:, None] == jnp.arange(total_angles, dtype=jnp.int32)[None, :]).astype(jnp.float32)
-    own_both = jnp.concatenate([own_real, own_imag], axis=1)
     pair_both = jnp.dot(swap, own_both, precision=highest)
     pair_real = pair_both[:, :columns]
     pair_imag = pair_both[:, columns:]

time: 98.2 us -> 93.4 us (0.951)
  local copies, waits for them, and re-layouts: 17.5 us -> 12.4 us
  waiting for transfers between devices: 7.94 us -> 10.3 us
  starting transfers between devices: 18.6 us -> 17.6 us
    slice x3 -> x0, local copies, waits for them, and re-layouts: 2.84 us -> none  [the longest x1 1.82 us: step_body(): own_imag = freq_major[1]]
    all_to_all x1, waiting for transfers between devices: 7.93 us -> 10.3 us  [step_body(): received = lax.all_to_all(payload, ANG_SL, 0, 0, tiled=True)]
    all_to_all x1 -> x0, other arithmetic: 1.57 us -> none  [step_body(): received = lax.all_to_all(payload, ANG_SL, 0, 0, tiled=True)]
    squeeze x2 -> x0, local copies, waits for them, and re-layouts: 1.32 us -> none  [the longest x1 1.13 us: step_body(): own_imag = freq_major[1]]
    all_to_all x1, starting transfers between devices: 10.9 us -> 9.86 us  [step_body(): received = lax.all_to_all(payload, ANG_SL, 0, 0, tiled=True)]
where the time goes in v1:
time: 93.4 us; the launch traced here: 93 us
  blocking collectives  18.7 us (20%)
  starting transfers between devices  17.6 us (19%)
  other arithmetic  16.1 us (17%)
  matrix products  15.6 us (17%)
  local copies, waits for them, and re-layouts  12.4 us (13%)
  waiting for transfers between devices  10.3 us (11%)
  between operations  2.32 us (2%)
    all_to_all x1, blocking collectives, step_body(): received = lax.all_to_all(payload, ANG_SL, 0, 0, tiled=True)  18.7 us
    all_to_all x1, waiting for transfers between devices, step_body(): received = lax.all_to_all(payload, ANG_SL, 0, 0, tiled=True)  10.3 us
    all_to_all x1, starting transfers between devices, step_body(): received = lax.all_to_all(payload, ANG_SL, 0, 0, tiled=True)  9.86 us
    ppermute x1, starting transfers between devices, from_behind(): return lax.ppermute(value, axis, pairs)  7.73 us
    mul x1, other arithmetic, step_body(): jnp.cos(phase_tab) * norm_scale  5.36 us
    dot_general x1, matrix products, step_body(): lax.dot_general(tabs, tabs, (((1,), (1,)), ((), ())), precision=highest)  5.28 us
    transpose x1, local copies, waits for them, and re-layouts, step_body(): payload = spectra.transpose(2, 3, 0, 1, 4).reshape(dev_count, -1)  3.99 us
    all_to_all x1, local copies, waits for them, and re-layouts, step_body(): received = lax.all_to_all(payload, ANG_SL, 0, 0, tiled=True)  3.06 us
  transfers between devices with their start and end apart: 2, of which 1 were waited for; matrix products, arithmetic and copies ran while one was open for 20% of the time, Pallas kernels for 0%

profile of v1, /device:TPU:1, one launch (start us, length us, event | category | flops | bytes accessed | tf_op | source)
XLA Modules:
  0.0 93.0 jit_solution(6985778121717180733)
XLA Ops:
  0.6 0.7 slice.70
  1.3 7.7 %collective-permute-start = (f32[2,4,256]{2,1,0:T(4,128)S(1)}, f32[2,4,256]{2,1,0:T(4,128)S(1)}, u32[]{:S(2)}, u32[]{:S(2)}) collective-permute-start(f32[2,4,256]{2,1,0:T(4,128)S(1)} %slice.70), channel_id=1, source_target_pairs={{0,128},{2,130},{4,132},{6,134},{8,136},{10,138},{12,140},{14,142}... | collective-permute-start | bytes 24584 | tf_op jit(solution)/shard_map/ppermute | solution.py:28
  9.3 0.8 compare_and_fusion
  10.1 0.7 convert_element_type.76
  11.2 0.9 multiply_bitcast_fusion
  12.0 5.4 %fusion.2 = (f32[256,1280]{1,0:T(8,128)S(1)}, f32[256,1280]{1,0:T(8,128)S(1)}) fusion(f32[1280]{0:T(1024)S(1)} %add_convert_fusion, f32[256]{0:T(256)} %param.8), kind=kLoop, calls=%fused_computation.7 | loop fusion | flops 983040 | bytes 2627584 | tf_op jit(solution)/shard_map/mul | solution.py:162
  17.4 5.3 %fusion = f32[512,512]{0,1:T(8,128)} fusion(f32[256,1280]{1,0:T(8,128)S(1)} %get-tuple-element.11, f32[256,1280]{1,0:T(8,128)S(1)} %get-tuple-element.10), kind=kOutput, calls=%fused_computation.5 | convolution fusion | flops 4027187200 | bytes 3670016 | tf_op jit(solution)/shard_map/dot_general | solution.py:189
  23.9 0.6 convolution_negate_fusion
  24.6 0.6 fusion.60
  26.3 1.0 %copy.36 = f32[8,32,128]{1,2,0:T(8,128)} copy(f32[8,32,128]{2,1,0:T(8,128)S(1)} %fusion.5) | data formatting | bytes 262144 | tf_op jit(solution)/shard_map/add | solution.py:89
  28.0 2.1 %maximum_bitcast_fusion = f32[32,8,2,8,16]{0,4,1,3,2:T(8,128)} fusion(f32[1,8,32,8,16]{2,4,3,1,0:T(8,128)S(1)} %bitcast.65, f32[1,8,32,8,16]{2,4,3,1,0:T(8,128)} %bitcast.64), kind=kLoop, calls=%fused_computation.19 | loop fusion | flops 65536 | bytes 524288 | tf_op jit(solution)/shard_map/transpose | solution.py:120
  30.1 4.0 %copy.38 = f32[32,8,2,8,16]{4,3,2,1,0:T(8,128)} copy(f32[32,8,2,8,16]{0,4,1,3,2:T(8,128)} %maximum_bitcast_fusion) | data formatting | bytes 524288 | tf_op jit(solution)/shard_map/transpose | solution.py:120
  34.1 3.1 %all_to_all.19 = f32[256,1,256]{2,1,0:T(1,128)} reshape(f32[32,8,2,8,16]{4,3,2,1,0:T(8,128)} %copy.38) | data formatting | bytes 524288 | tf_op jit(solution)/shard_map/all_to_all | solution.py:121
  37.1 9.9 %all-to-all-start = ((f32[256,1,256]{2,1,0:T(1,128)}), f32[256,1,256]{2,1,0:T(1,128)S(1)}, u32[]{:S(2)}, u32[]{:S(2)}) async-start(f32[256,1,256]{2,1,0:T(1,128)} %all_to_all.19), calls=%async_computation | async-start | bytes 524288 | tf_op jit(solution)/shard_map/all_to_all | solution.py:121
  47.5 2.2 %fusion.156 = (f32[256,256]{0,1:T(8,128)}, f32[256,256]{0,1:T(8,128)}, f32[256,256]{0,1:T(8,128)}) fusion(f32[512,512]{0,1:T(8,128)} %fusion), kind=kLoop, calls=%fused_computation.219 | loop fusion | flops 196608 | bytes 1835008 | tf_op jit(solution)/shard_map/neg | solution.py:194
  49.7 2.5 %fusion.1 = f32[512,256]{0,1:T(8,128)S(1)} fusion(f32[256,1280]{1,0:T(8,128)S(1)} %bitcast.63, f32[256,1280]{1,0:T(8,128)S(1)} %get-tuple-element.11, f32[256,1280]{1,0:T(8,128)S(1)} %get-tuple-element.10), kind=kOutput, calls=%fused_computation.6 | convolution fusion | flops 2013921280 | bytes 4456448 | tf_op jit(solution)/shard_map/dot_general | solution.py:166
  52.2 10.3 %all-to-all-done = f32[256,1,256]{2,1,0:T(1,128)S(1)} async-done(((f32[256,1,256]{2,1,0:T(1,128)}), f32[256,1,256]{2,1,0:T(1,128)S(1)}, u32[]{:S(2)}, u32[]{:S(2)}) %all-to-all-start) | async-done | bytes 262176 | tf_op jit(solution)/shard_map/all_to_all | solution.py:121
  64.4 0.7 fusion.7
  65.1 0.7 add_reduce_fusion
  66.5 1.4 %pad_maximum_fusion.6 = f32[10]{0:T(128)S(1)} fusion(f32[1]{0:T(128)} %bitcast.17, f32[1]{0:T(128)} %bitcast.16), kind=kLoop, calls=%fused_computation.175 | loop fusion | flops 10 | bytes 48 | tf_op jit(solution)/shard_map/stack | solution.py:205
  67.9 18.7 %all_to_all.22 = f32[256,1,10]{2,1,0:T(1,128)S(1)} all-to-all(f32[256,1,10]{2,1,0:T(1,128)S(1)} %bitcast.67), channel_id=1, replica_groups=mesh['ang_0'=8,'ang_1'=2,'ang_2'=4,'ang_3'=2,'sl'=2] {'ang_0','ang_1','a..., dimensions={0} | all-to-all | bytes 20480 | tf_op jit(solution)/shard_map/all_to_all | solution.py:207
  88.8 2.3 %convolution_multiply_fusion = f32[256,1280]{1,0:T(8,128)S(1)} fusion(f32[256,1280]{1,0:T(8,128)S(1)} %get-tuple-element.11, f32[256,1280]{1,0:T(8,128)S(1)} %get-tuple-element.10, f32[]{:T(128)} %bitcast.20, f32[256,128]{0,1:T(8,128)S(1)} %get-tuple-element.9, f32[256,128]{0,1:T(8,128)S(1)} %get-tuple-element.15, f32[256,128]{0,1:T(8,128)S(1)} %get-tuple-element.14), kind=kOutput, calls=%fused_computation.1 | convolution fusion | flops 2014642176 | bytes 4325380 | tf_op jit(solution)/shard_map/dot_general | solution.py:211
  91.1 1.2 %sub.107 = f32[2,8,16,1280]{3,2,1,0:T(8,128)} subtract(f32[2,8,16,1280]{3,2,1,0:T(8,128)S(1)} %copy-done.1, f32[2,8,16,1280]{3,2,1,0:T(8,128)S(1)} %bitcast.62) | non-fusion elementwise | flops 327680 | bytes 3932160 | tf_op jit(solution)/shard_map/sub | solution.py:212
  92.3 0.6 reshape.265
  (66 shorter events, 7.3 us)
Async XLA Ops:
  1.3 21.4 %collective-permute-start = (f32[2,4,256]{2,1,0:T(4,128)S(1)}, f32[2,4,256]{2,1,0:T(4,128)S(1)}, u32[]{:S(2)}, u32[]{:S(2)}) collective-permute-start(f32[2,4,256]{2,1,0:T(4,128)S(1)} %slice.70), channel_id=1, source_target_pairs={{0,128},{2,130},{4,132},{6,134},{8,136},{10,138},{12,140},{14,142}... | collective-permute-start | bytes 24584 | tf_op jit(solution)/shard_map/ppermute | solution.py:28
  17.4 6.3 %copy-start.3 = (f32[2,4,4352]{2,1,0:T(4,128)S(1)}, f32[2,4,4352]{2,1,0:T(4,128)}, u32[]{:S(2)}) copy-start(f32[2,4,4352]{2,1,0:T(4,128)} %param.5) | copy-start | bytes 417796
  17.4 6.3 %slice-start = ((f32[2,4,4352]{2,1,0:T(4,128)}), f32[2,4,3840]{2,1,0:T(4,128)S(1)}, s32[]{:S(2)}) async-start(f32[2,4,4352]{2,1,0:T(4,128)} %param.5), calls=%async_computation.2 | async-start | bytes 245760 | tf_op jit(solution)/shard_map/slice | solution.py:55
  34.1 13.0 %copy-start.2 = (f32[8,16,8,16]{3,2,1,0:T(8,128)S(1)}, f32[8,16,8,16]{3,2,1,0:T(8,128)}, u32[]{:S(2)}) copy-start(f32[8,16,8,16]{3,2,1,0:T(8,128)} %multiply_bitcast_fusion) | copy-start | bytes 196612
  37.1 25.4 %all-to-all-start = ((f32[256,1,256]{2,1,0:T(1,128)}), f32[256,1,256]{2,1,0:T(1,128)S(1)}, u32[]{:S(2)}, u32[]{:S(2)}) async-start(f32[256,1,256]{2,1,0:T(1,128)} %all_to_all.19), calls=%async_computation | async-start | bytes 524288 | tf_op jit(solution)/shard_map/all_to_all | solution.py:121
  47.5 2.2 %copy-start = (f32[2,8,16,1280]{3,2,1,0:T(8,128)S(1)}, f32[2,8,16,1280]{3,2,1,0:T(8,128)}, u32[]{:S(2)}) copy-start(f32[2,8,16,1280]{3,2,1,0:T(8,128)} %param.9) | copy-start | bytes 3932164
  52.2 11.0 %copy-start.7 = (s32[256]{0:T(256)S(1)}, s32[256]{0:T(256)}, u32[]{:S(2)}) copy-start(s32[256]{0:T(256)} %param.6) | copy-start | bytes 3076
  63.2 1.1 %copy-start.4 = (f32[256,256]{0,1:T(8,128)S(1)}, f32[256,256]{0,1:T(8,128)}, u32[]{:S(2)}) copy-start(f32[256,256]{0,1:T(8,128)} %get-tuple-element.4) | copy-start | bytes 786436
  63.2 1.1 %copy-start.5 = (f32[256,256]{0,1:T(8,128)S(1)}, f32[256,256]{0,1:T(8,128)}, u32[]{:S(2)}) copy-start(f32[256,256]{0,1:T(8,128)} %get-tuple-element.5) | copy-start | bytes 786436
  63.2 1.1 %copy-start.6 = (f32[256,256]{0,1:T(8,128)S(1)}, f32[256,256]{0,1:T(8,128)}, u32[]{:S(2)}) copy-start(f32[256,256]{0,1:T(8,128)} %get-tuple-element.8) | copy-start | bytes 786436
  88.8 2.3 %copy-start.1 = (f32[2,8,16,1280]{3,2,1,0:T(8,128)S(1)}, f32[2,8,16,1280]{3,2,1,0:T(8,128)}, u32[]{:S(2)}) copy-start(f32[2,8,16,1280]{3,2,1,0:T(8,128)} %param.9) | copy-start | bytes 3932164

commit v2 on v1

--- a/solution.py
+++ b/solution.py
@@ -196,7 +196,7 @@
         ]
     )
     resid_both = jnp.concatenate([resid_real, resid_imag])
-    image_both = jnp.dot(gram_both, resid_both, precision=highest)
+    image_both = jnp.dot(gram_both, resid_both, precision=lax.Precision.HIGH)
     image_real, image_imag = image_both[:total_angles], image_both[total_angles:]
     curvature = jnp.sum(ramp_weights * (image_real * image_real + image_imag * image_imag))
     grad_norm = jnp.sum(resid_real * image_real + resid_imag * image_imag)
@@ -208,8 +208,10 @@
     totals = jnp.sum(received, axis=0)
     misfit = totals[: per_dev * rows_dev].reshape(per_dev, rows_dev)
     step_size = totals[per_dev * rows_dev] / (totals[per_dev * rows_dev + 1] + small_eps)
-    grad = lax.dot_general(stacked, tabs, (((0,), (0,)), ((), ())), precision=highest)
-    updated = coefficients - step_size * grad.reshape(coefficients.shape)
+    step_grad = lax.dot_general(
+        -step_size * stacked, tabs, (((0,), (0,)), ((), ())), precision=lax.Precision.HIGH
+    )
+    updated = coefficients + step_grad.reshape(coefficients.shape)
     return (updated, misfit)
 
 

time: 93.4 us -> 92.5 us (level)
  matrix products: 15.6 us -> 14.3 us
    dot_general x2, matrix products: 3.02 us -> 1.79 us  [the longest x1 1.35 us: step_body(): lax.dot_general(-step_size * stacked, tabs, (((0,), (0,)), ((), ())), pre...]
    add x0 -> x1, other arithmetic: none -> 1.19 us  [step_body(): updated = coefficients + step_grad.reshape(coefficients.shape)]
    sub x1 -> x0, other arithmetic: 1.19 us -> none  [step_body(): updated = coefficients - step_size * grad.reshape(coefficients.shape)]
where the time goes in v2:
time: 92.5 us; the launch traced here: 92 us
  blocking collectives  19 us (21%)
  starting transfers between devices  17.6 us (19%)
  other arithmetic  16.1 us (17%)
  matrix products  14.3 us (15%)
  local copies, waits for them, and re-layouts  12.5 us (14%)
  waiting for transfers between devices  10.3 us (11%)
  between operations  2.34 us (3%)
    all_to_all x1, blocking collectives, step_body(): received = lax.all_to_all(payload, ANG_SL, 0, 0, tiled=True)  19 us
    all_to_all x1, waiting for transfers between devices, step_body(): received = lax.all_to_all(payload, ANG_SL, 0, 0, tiled=True)  10.3 us
    all_to_all x1, starting transfers between devices, step_body(): received = lax.all_to_all(payload, ANG_SL, 0, 0, tiled=True)  9.84 us
    ppermute x1, starting transfers between devices, from_behind(): return lax.ppermute(value, axis, pairs)  7.73 us
    mul x1, other arithmetic, step_body(): jnp.cos(phase_tab) * norm_scale  5.36 us
    dot_general x1, matrix products, step_body(): lax.dot_general(tabs, tabs, (((1,), (1,)), ((), ())), precision=highest)  5.28 us
    transpose x1, local copies, waits for them, and re-layouts, step_body(): payload = spectra.transpose(2, 3, 0, 1, 4).reshape(dev_count, -1)  3.99 us
    all_to_all x1, local copies, waits for them, and re-layouts, step_body(): received = lax.all_to_all(payload, ANG_SL, 0, 0, tiled=True)  3.06 us
  transfers between devices with their start and end apart: 2, of which 1 were waited for; matrix products, arithmetic and copies ran while one was open for 20% of the time, Pallas kernels for 0%

profile of v2, /device:TPU:1, one launch (start us, length us, event | category | flops | bytes accessed | tf_op | source)
XLA Modules:
  0.0 92.0 jit_solution(708845827702767276)
XLA Ops:
  0.6 0.7 slice.70
  1.3 7.7 %collective-permute-start = (f32[2,4,256]{2,1,0:T(4,128)S(1)}, f32[2,4,256]{2,1,0:T(4,128)S(1)}, u32[]{:S(2)}, u32[]{:S(2)}) collective-permute-start(f32[2,4,256]{2,1,0:T(4,128)S(1)} %slice.70), channel_id=1, source_target_pairs={{0,128},{2,130},{4,132},{6,134},{8,136},{10,138},{12,140},{14,142}... | collective-permute-start | bytes 24584 | tf_op jit(solution)/shard_map/ppermute | solution.py:28
  9.3 0.8 compare_and_fusion
  10.1 0.7 convert_element_type.76
  11.2 0.8 multiply_bitcast_fusion
  12.0 5.4 %fusion.3 = (f32[256,1280]{1,0:T(8,128)S(1)}, f32[256,1280]{1,0:T(8,128)S(1)}) fusion(f32[1280]{0:T(1024)S(1)} %add_convert_fusion, f32[256]{0:T(256)} %param.8), kind=kLoop, calls=%fused_computation.7 | loop fusion | flops 983040 | bytes 2627584 | tf_op jit(solution)/shard_map/mul | solution.py:162
  17.4 5.3 %fusion.1 = f32[512,512]{0,1:T(8,128)} fusion(f32[256,1280]{1,0:T(8,128)S(1)} %get-tuple-element.11, f32[256,1280]{1,0:T(8,128)S(1)} %get-tuple-element.10), kind=kOutput, calls=%fused_computation.5 | convolution fusion | flops 4027187200 | bytes 3670016 | tf_op jit(solution)/shard_map/dot_general | solution.py:189
  23.9 0.6 convolution_negate_fusion
  24.5 0.6 fusion.61
  26.3 1.0 %copy.36 = f32[8,32,128]{1,2,0:T(8,128)} copy(f32[8,32,128]{2,1,0:T(8,128)S(1)} %fusion.6) | data formatting | bytes 262144 | tf_op jit(solution)/shard_map/add | solution.py:89
  27.9 2.1 %maximum_bitcast_fusion = f32[32,8,2,8,16]{0,4,1,3,2:T(8,128)} fusion(f32[1,8,32,8,16]{2,4,3,1,0:T(8,128)S(1)} %bitcast.65, f32[1,8,32,8,16]{2,4,3,1,0:T(8,128)} %bitcast.64), kind=kLoop, calls=%fused_computation.19 | loop fusion | flops 65536 | bytes 524288 | tf_op jit(solution)/shard_map/transpose | solution.py:120
  30.0 4.0 %copy.38 = f32[32,8,2,8,16]{4,3,2,1,0:T(8,128)} copy(f32[32,8,2,8,16]{0,4,1,3,2:T(8,128)} %maximum_bitcast_fusion) | data formatting | bytes 524288 | tf_op jit(solution)/shard_map/transpose | solution.py:120
  34.0 3.1 %all_to_all.19 = f32[256,1,256]{2,1,0:T(1,128)} reshape(f32[32,8,2,8,16]{4,3,2,1,0:T(8,128)} %copy.38) | data formatting | bytes 524288 | tf_op jit(solution)/shard_map/all_to_all | solution.py:121
  37.1 9.8 %all-to-all-start = ((f32[256,1,256]{2,1,0:T(1,128)}), f32[256,1,256]{2,1,0:T(1,128)S(1)}, u32[]{:S(2)}, u32[]{:S(2)}) async-start(f32[256,1,256]{2,1,0:T(1,128)} %all_to_all.19), calls=%async_computation | async-start | bytes 524288 | tf_op jit(solution)/shard_map/all_to_all | solution.py:121
  47.5 2.2 %fusion.157 = (f32[256,256]{0,1:T(8,128)}, f32[256,256]{0,1:T(8,128)}, f32[256,256]{0,1:T(8,128)}) fusion(f32[512,512]{0,1:T(8,128)} %fusion.1), kind=kLoop, calls=%fused_computation.220 | loop fusion | flops 196608 | bytes 1835008 | tf_op jit(solution)/shard_map/neg | solution.py:194
  49.7 2.5 %fusion.2 = f32[512,256]{0,1:T(8,128)S(1)} fusion(f32[256,1280]{1,0:T(8,128)S(1)} %bitcast.63, f32[256,1280]{1,0:T(8,128)S(1)} %get-tuple-element.11, f32[256,1280]{1,0:T(8,128)S(1)} %get-tuple-element.10), kind=kOutput, calls=%fused_computation.6 | convolution fusion | flops 2013921280 | bytes 4456448 | tf_op jit(solution)/shard_map/dot_general | solution.py:166
  52.2 10.3 %all-to-all-done = f32[256,1,256]{2,1,0:T(1,128)S(1)} async-done(((f32[256,1,256]{2,1,0:T(1,128)}), f32[256,1,256]{2,1,0:T(1,128)S(1)}, u32[]{:S(2)}, u32[]{:S(2)}) %all-to-all-start) | async-done | bytes 262176 | tf_op jit(solution)/shard_map/all_to_all | solution.py:121
  64.8 0.8 add_reduce_fusion
  66.3 1.3 %pad_maximum_fusion.6 = f32[10]{0:T(128)S(1)} fusion(f32[1]{0:T(128)} %bitcast.17, f32[1]{0:T(128)} %bitcast.16), kind=kLoop, calls=%fused_computation.176 | loop fusion | flops 10 | bytes 48 | tf_op jit(solution)/shard_map/stack | solution.py:205
  67.6 19.0 %all_to_all.22 = f32[256,1,10]{2,1,0:T(1,128)S(1)} all-to-all(f32[256,1,10]{2,1,0:T(1,128)S(1)} %bitcast.67), channel_id=1, replica_groups=mesh['ang_0'=8,'ang_1'=2,'ang_2'=4,'ang_3'=2,'sl'=2] {'ang_0','ang_1','a..., dimensions={0} | all-to-all | bytes 20480 | tf_op jit(solution)/shard_map/all_to_all | solution.py:207
  86.9 0.7 fusion.158
  88.8 1.4 %fusion = f32[256,1280]{1,0:T(8,128)S(1)} fusion(f32[256,1280]{1,0:T(8,128)S(1)} %get-tuple-element.11, f32[256,1280]{1,0:T(8,128)S(1)} %get-tuple-element.10, f32[256,128]{0,1:T(8,128)S(1)} %get-tuple-element.9, f32[256,128]{0,1:T(8,128)S(1)} %copy-done.6, f32[256,128]{0,1:T(8,128)S(1)} %copy-done.4, f32[]{:T(128)} %bitcast.20), kind=kOutput, calls=%fused_computation.4 | convolution fusion | flops 1007812608 | bytes 4325380 | tf_op jit(solution)/shard_map/dot_general | solution.py:211
  90.2 1.2 %add.215 = f32[2,8,16,1280]{3,2,1,0:T(8,128)} add(f32[2,8,16,1280]{3,2,1,0:T(8,128)S(1)} %copy-done.1, f32[2,8,16,1280]{3,2,1,0:T(8,128)S(1)} %bitcast.62) | non-fusion elementwise | flops 327680 | bytes 3932160 | tf_op jit(solution)/shard_map/add | solution.py:214
  91.4 0.6 reshape.267
  (74 shorter events, 7.2 us)
Async XLA Ops:
  1.3 21.4 %collective-permute-start = (f32[2,4,256]{2,1,0:T(4,128)S(1)}, f32[2,4,256]{2,1,0:T(4,128)S(1)}, u32[]{:S(2)}, u32[]{:S(2)}) collective-permute-start(f32[2,4,256]{2,1,0:T(4,128)S(1)} %slice.70), channel_id=1, source_target_pairs={{0,128},{2,130},{4,132},{6,134},{8,136},{10,138},{12,140},{14,142}... | collective-permute-start | bytes 24584 | tf_op jit(solution)/shard_map/ppermute | solution.py:28
  17.4 6.3 %copy-start.7 = (f32[2,4,4352]{2,1,0:T(4,128)S(1)}, f32[2,4,4352]{2,1,0:T(4,128)}, u32[]{:S(2)}) copy-start(f32[2,4,4352]{2,1,0:T(4,128)} %param.5) | copy-start | bytes 417796
  17.4 6.3 %slice-start = ((f32[2,4,4352]{2,1,0:T(4,128)}), f32[2,4,3840]{2,1,0:T(4,128)S(1)}, s32[]{:S(2)}) async-start(f32[2,4,4352]{2,1,0:T(4,128)} %param.5), calls=%async_computation.2 | async-start | bytes 245760 | tf_op jit(solution)/shard_map/slice | solution.py:55
  34.0 13.0 %copy-start.2 = (f32[8,16,8,16]{3,2,1,0:T(8,128)S(1)}, f32[8,16,8,16]{3,2,1,0:T(8,128)}, u32[]{:S(2)}) copy-start(f32[8,16,8,16]{3,2,1,0:T(8,128)} %multiply_bitcast_fusion) | copy-start | bytes 196612
  37.1 25.4 %all-to-all-start = ((f32[256,1,256]{2,1,0:T(1,128)}), f32[256,1,256]{2,1,0:T(1,128)S(1)}, u32[]{:S(2)}, u32[]{:S(2)}) async-start(f32[256,1,256]{2,1,0:T(1,128)} %all_to_all.19), calls=%async_computation | async-start | bytes 524288 | tf_op jit(solution)/shard_map/all_to_all | solution.py:121
  47.5 2.2 %copy-start = (f32[2,8,16,1280]{3,2,1,0:T(8,128)S(1)}, f32[2,8,16,1280]{3,2,1,0:T(8,128)}, u32[]{:S(2)}) copy-start(f32[2,8,16,1280]{3,2,1,0:T(8,128)} %param.9) | copy-start | bytes 3932164
  52.2 11.0 %copy-start.11 = (s32[256]{0:T(256)S(1)}, s32[256]{0:T(256)}, u32[]{:S(2)}) copy-start(s32[256]{0:T(256)} %param.6) | copy-start | bytes 3076
  63.2 1.2 %copy-start.8 = (f32[256,256]{0,1:T(8,128)S(1)}, f32[256,256]{0,1:T(8,128)}, u32[]{:S(2)}) copy-start(f32[256,256]{0,1:T(8,128)} %get-tuple-element.4) | copy-start | bytes 786436
  63.2 1.2 %copy-start.9 = (f32[256,256]{0,1:T(8,128)S(1)}, f32[256,256]{0,1:T(8,128)}, u32[]{:S(2)}) copy-start(f32[256,256]{0,1:T(8,128)} %get-tuple-element.5) | copy-start | bytes 786436
  63.2 1.2 %copy-start.10 = (f32[256,256]{0,1:T(8,128)S(1)}, f32[256,256]{0,1:T(8,128)}, u32[]{:S(2)}) copy-start(f32[256,256]{0,1:T(8,128)} %get-tuple-element.8) | copy-start | bytes 786436
  64.2 1.4 %copy-start.3 = (f32[256,128]{0,1:T(8,128)}, f32[256,128]{0,1:T(8,128)S(1)}, u32[]{:S(2)}) copy-start(f32[256,128]{0,1:T(8,128)S(1)} %get-tuple-element.14) | copy-start | bytes 393220
  64.2 1.4 %copy-start.5 = (f32[256,128]{0,1:T(8,128)}, f32[256,128]{0,1:T(8,128)S(1)}, u32[]{:S(2)}) copy-start(f32[256,128]{0,1:T(8,128)S(1)} %get-tuple-element.15) | copy-start | bytes 393220
  65.6 23.2 %copy-start.4 = (f32[256,128]{0,1:T(8,128)S(1)}, f32[256,128]{0,1:T(8,128)}, u32[]{:S(2)}) copy-start(f32[256,128]{0,1:T(8,128)} %copy-done.3) | copy-start | bytes 393220
  65.6 23.2 %copy-start.6 = (f32[256,128]{0,1:T(8,128)S(1)}, f32[256,128]{0,1:T(8,128)}, u32[]{:S(2)}) copy-start(f32[256,128]{0,1:T(8,128)} %copy-done.5) | copy-start | bytes 393220
  88.8 1.4 %copy-start.1 = (f32[2,8,16,1280]{3,2,1,0:T(8,128)S(1)}, f32[2,8,16,1280]{3,2,1,0:T(8,128)}, u32[]{:S(2)}) copy-start(f32[2,8,16,1280]{3,2,1,0:T(8,128)} %param.9) | copy-start | bytes 3932164

commit v3 on v2

--- a/solution.py
+++ b/solution.py
@@ -110,7 +110,10 @@
     across_dev = (ang_index + ang_count // 2) % ang_count
     partner_slots = own_partners - across_dev * per_dev
     arrived = from_behind(projections[:, :, HALF:], ANG, ang_count // 2)
-    mirrored = jnp.flip(jnp.take(arrived, partner_slots, axis=0), axis=2)
+    chosen = arrived[0]
+    for slot in range(1, per_dev):
+        chosen = jnp.where((partner_slots == slot)[:, None, None], arrived[slot], chosen)
+    mirrored = jnp.flip(chosen, axis=2)
     stitched = blend_band(projections, mirrored, offsets)
     spec_real, spec_imag = spectrum_of(stitched)
     spectra = jnp.stack([spec_real, spec_imag])
@@ -202,16 +205,24 @@
     grad_norm = jnp.sum(resid_real * image_real + resid_imag * image_imag)
     by_owner = misfit_table.reshape(ang_count, per_dev, sl_count, rows_dev)
     by_owner = jnp.swapaxes(by_owner, 1, 2).reshape(ang_count * sl_count, per_dev * rows_dev)
-    scalars = jnp.broadcast_to(jnp.stack([grad_norm, curvature])[None], (ang_count * sl_count, 2))
-    payload = jnp.concatenate([by_owner, scalars], axis=1)
+    owners = ang_count * sl_count
+    payload = jnp.concatenate(
+        [
+            by_owner,
+            jnp.broadcast_to(grad_norm, (owners, 1)),
+            jnp.broadcast_to(curvature, (owners, 1)),
+        ],
+        axis=1,
+    )
+    grad = lax.dot_general(
+        stacked, tabs, (((0,), (0,)), ((), ())), precision=lax.Precision.HIGH
+    )
+    grad = lax.optimization_barrier(grad.reshape(coefficients.shape))
     received = lax.all_to_all(payload, ANG_SL, 0, 0, tiled=True)
     totals = jnp.sum(received, axis=0)
     misfit = totals[: per_dev * rows_dev].reshape(per_dev, rows_dev)
     step_size = totals[per_dev * rows_dev] / (totals[per_dev * rows_dev + 1] + small_eps)
-    step_grad = lax.dot_general(
-        -step_size * stacked, tabs, (((0,), (0,)), ((), ())), precision=lax.Precision.HIGH
-    )
-    updated = coefficients + step_grad.reshape(coefficients.shape)
+    updated = coefficients - step_size * grad
     return (updated, misfit)
 
 

time: 92.5 us -> 96 us (1.038)
  blocking collectives: 19 us -> 0 us
  waiting for transfers between devices: 10.3 us -> 20.9 us
  starting transfers between devices: 17.6 us -> 23.8 us
  matrix products: 14.3 us -> 17.2 us
  local copies, waits for them, and re-layouts: 12.5 us -> 15 us
    all_to_all x1 -> x0, blocking collectives: 19 us -> none  [step_body(): received = lax.all_to_all(payload, ANG_SL, 0, 0, tiled=True)]
    all_to_all x1 -> x2, waiting for transfers between devices: 10.3 us -> 20.9 us  [step_body(): received = lax.all_to_all(payload, ANG_SL, 0, 0, tiled=True)]
    all_to_all x1 -> x2, starting transfers between devices: 9.84 us -> 16.1 us  [step_body(): received = lax.all_to_all(payload, ANG_SL, 0, 0, tiled=True)]
    sub x0 -> x1, other arithmetic: none -> 2.91 us  [step_body(): updated = coefficients - step_size * grad]
    concatenate x0 -> x2, local copies, waits for them, and re-layouts: none -> 1.44 us  [step_body(): jnp.concatenate([by_owner, jnp.broadcast_to(grad_norm, (owners, 1)), jnp....]
    another operation x2 -> x1, other arithmetic: 1.34 us -> 0.01 us  [the longest x1 1.34 us: step_body(): jnp.stack([grad_norm, curvature])[None]]
    dot_general x1, matrix products: 0.43 us -> 1.67 us  [step_body(): image_both = jnp.dot(gram_both, resid_both, precision=lax.Precision.HIGH)]
    add x1 -> x0, other arithmetic: 1.19 us -> none  [step_body(): updated = coefficients + step_grad.reshape(coefficients.shape)]
  transfers between devices with their start and end apart: 2 -> 3, of which waited for: 1 -> 2; matrix products, arithmetic and copies ran while one was open for 20% -> 21% of each run, Pallas kernels for 0% -> 0%
where the time goes in v3:
time: 96 us; the launch traced here: 95.5 us
  starting transfers between devices  23.8 us (25%)
  waiting for transfers between devices  20.9 us (22%)
  matrix products  17.2 us (18%)
  other arithmetic  16.4 us (17%)
  local copies, waits for them, and re-layouts  15 us (16%)
  between operations  2.21 us (2%)
    all_to_all x2, waiting for transfers between devices, step_body(): received = lax.all_to_all(payload, ANG_SL, 0, 0, tiled=True)  20.9 us
    all_to_all x2, starting transfers between devices, step_body(): received = lax.all_to_all(payload, ANG_SL, 0, 0, tiled=True)  16.1 us
    ppermute x1, starting transfers between devices, from_behind(): return lax.ppermute(value, axis, pairs)  7.73 us
    mul x1, other arithmetic, step_body(): jnp.cos(phase_tab) * norm_scale  5.36 us
    dot_general x1, matrix products, step_body(): lax.dot_general(tabs, tabs, (((1,), (1,)), ((), ())), precision=highest)  5.28 us
    transpose x1, local copies, waits for them, and re-layouts, step_body(): payload = spectra.transpose(2, 3, 0, 1, 4).reshape(dev_count, -1)  3.99 us
    all_to_all x1, local copies, waits for them, and re-layouts, step_body(): received = lax.all_to_all(payload, ANG_SL, 0, 0, tiled=True)  3 us
    sub x1, other arithmetic, step_body(): updated = coefficients - step_size * grad  2.91 us
  transfers between devices with their start and end apart: 3, of which 2 were waited for; matrix products, arithmetic and copies ran while one was open for 21% of the time, Pallas kernels for 0%

profile of v3, /device:TPU:1, one launch (start us, length us, event | category | flops | bytes accessed | tf_op | source)
XLA Modules:
  0.0 95.5 jit_solution(3575435862883627775)
XLA Ops:
  0.6 0.7 slice.76
  1.3 7.7 %collective-permute-start = (f32[2,4,256]{2,1,0:T(4,128)S(1)}, f32[2,4,256]{2,1,0:T(4,128)S(1)}, u32[]{:S(2)}, u32[]{:S(2)}) collective-permute-start(f32[2,4,256]{2,1,0:T(4,128)S(1)} %slice.76), channel_id=1, source_target_pairs={{0,128},{2,130},{4,132},{6,134},{8,136},{10,138},{12,140},{14,142}... | collective-permute-start | bytes 24584 | tf_op jit(solution)/shard_map/ppermute | solution.py:28
  10.4 5.4 %fusion.3 = (f32[256,1280]{1,0:T(8,128)S(1)}, f32[256,1280]{1,0:T(8,128)S(1)}) fusion(f32[1280]{0:T(1024)S(1)} %add_convert_fusion, f32[256]{0:T(256)} %param.8), kind=kLoop, calls=%fused_computation.6 | loop fusion | flops 983040 | bytes 2627584 | tf_op jit(solution)/shard_map/mul | solution.py:165
  15.8 5.3 %fusion.1 = f32[512,512]{0,1:T(8,128)} fusion(f32[256,1280]{1,0:T(8,128)S(1)} %get-tuple-element.9, f32[256,1280]{1,0:T(8,128)S(1)} %get-tuple-element.8), kind=kOutput, calls=%fused_computation.4 | convolution fusion | flops 4027187200 | bytes 3670016 | tf_op jit(solution)/shard_map/dot_general | solution.py:192
  21.6 0.7 pad_maximum_fusion.4
  22.3 1.1 %reshape.256 = f32[8,64,64]{2,1,0:T(8,128)S(1)} reshape(f32[2,4,4096]{2,1,0:T(4,128)} %pad_maximum_fusion.4) | data formatting | bytes 262144 | tf_op jit(solution)/shard_map/reshape | solution.py:63
  26.2 1.0 %copy.36 = f32[8,32,128]{1,2,0:T(8,128)} copy(f32[8,32,128]{2,1,0:T(8,128)S(1)} %fusion.6) | data formatting | bytes 262144 | tf_op jit(solution)/shard_map/add | solution.py:89
  27.2 1.0 %copy.37 = f32[8,32,128]{1,2,0:T(8,128)} copy(f32[8,32,128]{2,1,0:T(8,128)S(1)} %fusion.5) | data formatting | bytes 262144 | tf_op jit(solution)/shard_map/sub | solution.py:92
  28.2 2.3 %maximum_bitcast_fusion = f32[32,8,2,8,16]{0,4,1,3,2:T(8,128)} fusion(f32[1,8,32,8,16]{2,4,3,1,0:T(8,128)} %bitcast.69, f32[1,8,32,8,16]{2,4,3,1,0:T(8,128)} %bitcast.68), kind=kLoop, calls=%fused_computation.19 | loop fusion | flops 65536 | bytes 524288 | tf_op jit(solution)/shard_map/transpose | solution.py:123
  30.5 4.0 %copy.38 = f32[32,8,2,8,16]{4,3,2,1,0:T(8,128)} copy(f32[32,8,2,8,16]{0,4,1,3,2:T(8,128)} %maximum_bitcast_fusion) | data formatting | bytes 524288 | tf_op jit(solution)/shard_map/transpose | solution.py:123
  34.5 3.0 %all_to_all.19 = f32[256,1,256]{2,1,0:T(1,128)} reshape(f32[32,8,2,8,16]{4,3,2,1,0:T(8,128)} %copy.38) | data formatting | bytes 524288 | tf_op jit(solution)/shard_map/all_to_all | solution.py:124
  37.5 9.8 %all-to-all-start = ((f32[256,1,256]{2,1,0:T(1,128)}), f32[256,1,256]{2,1,0:T(1,128)S(1)}, u32[]{:S(2)}, u32[]{:S(2)}) async-start(f32[256,1,256]{2,1,0:T(1,128)} %all_to_all.19), calls=%async_computation | async-start | bytes 524288 | tf_op jit(solution)/shard_map/all_to_all | solution.py:124
  47.9 2.2 %fusion.157 = (f32[256,256]{0,1:T(8,128)}, f32[256,256]{0,1:T(8,128)}, f32[256,256]{0,1:T(8,128)}) fusion(f32[512,512]{0,1:T(8,128)} %fusion.1), kind=kLoop, calls=%fused_computation.218 | loop fusion | flops 196608 | bytes 1835008 | tf_op jit(solution)/shard_map/neg | solution.py:197
  50.1 2.5 %fusion.2 = f32[512,256]{0,1:T(8,128)S(1)} fusion(f32[256,1280]{1,0:T(8,128)S(1)} %bitcast.67, f32[256,1280]{1,0:T(8,128)S(1)} %get-tuple-element.9, f32[256,1280]{1,0:T(8,128)S(1)} %get-tuple-element.8), kind=kOutput, calls=%fused_computation.5 | convolution fusion | flops 2013921280 | bytes 4456448 | tf_op jit(solution)/shard_map/dot_general | solution.py:169
  52.6 10.3 %all-to-all-done = f32[256,1,256]{2,1,0:T(1,128)S(1)} async-done(((f32[256,1,256]{2,1,0:T(1,128)}), f32[256,1,256]{2,1,0:T(1,128)S(1)}, u32[]{:S(2)}, u32[]{:S(2)}) %all-to-all-start) | async-done | bytes 262176 | tf_op jit(solution)/shard_map/all_to_all | solution.py:124
  64.2 1.0 %broadcast_multiply_fusion.1 = (f32[256,128]{0,1:T(8,128)}, f32[256,128]{0,1:T(8,128)}, f32[256,128]{0,1:T(8,128)S(1)}) fusion(f32[128]{0:T(128)S(1)} %div.62, f32[256,128]{0,1:T(8,128)S(1)} %convolution_subtract_fusion, f32[128,128]{1,0:T(8,128)S(1)} %reshape.257, f32[256,256]{1,0:T(8,128)S(1)} %convolution_select_fusion, f32[256,256]{1,0:T(8,128)S(1)} %fusion.28, ...), kind=kOutput, calls=%fused_computation.74 | convolution fusion | flops 50593792 | bytes 1246720 | tf_op jit(solution)/shard_map/dot_general | solution.py:157
  66.1 1.7 %fusion.8 = f32[512,128]{0,1:T(8,128)S(1)} fusion(f32[256,256]{0,1:T(8,128)} %get-tuple-element.6, f32[256,256]{0,1:T(8,128)} %get-tuple-element.5, f32[256,256]{0,1:T(8,128)} %get-tuple-element.4, f32[256,128]{0,1:T(8,128)} %get-tuple-element.15, f32[256,128]{0,1:T(8,128)S(1)} %copy-done.1), kind=kOutput, calls=%fused_computation.20 | convolution fusion | flops 202178560 | bytes 1310720 | tf_op jit(solution)/shard_map/dot_general | solution.py:202
  67.8 0.7 add_reduce_fusion
  68.5 0.7 pad.5.clone
  69.2 0.7 pad.6.clone
  70.6 6.2 %all-to-all-start.1 = ((f32[256,1,10]{2,1,0:T(1,128)}), f32[256,1,10]{2,1,0:T(1,128)S(1)}, u32[]{:S(2)}, u32[]{:S(2)}) async-start(f32[256,1,10]{2,1,0:T(1,128)} %bitcast.19), calls=%async_computation.1 | async-start | bytes 262144 | tf_op jit(solution)/shard_map/all_to_all | solution.py:221
  76.8 2.4 %fusion = f32[256,1280]{1,0:T(8,128)} fusion(f32[256,1280]{1,0:T(8,128)S(1)} %get-tuple-element.9, f32[256,1280]{1,0:T(8,128)S(1)} %get-tuple-element.8, f32[256,128]{0,1:T(8,128)S(1)} %get-tuple-element.7, f32[256,128]{0,1:T(8,128)S(1)} %copy-done.2, f32[256,128]{0,1:T(8,128)S(1)} %copy-done.1), kind=kOutput, calls=%fused_computation.3 | convolution fusion | flops 1007681536 | bytes 4325376 | tf_op jit(solution)/shard_map/dot_general | solution.py:217
  79.2 10.6 %all-to-all-done.1 = f32[256,1,10]{2,1,0:T(1,128)S(1)} async-done(((f32[256,1,10]{2,1,0:T(1,128)}), f32[256,1,10]{2,1,0:T(1,128)S(1)}, u32[]{:S(2)}, u32[]{:S(2)}) %all-to-all-start.1) | async-done | bytes 10272 | tf_op jit(solution)/shard_map/all_to_all | solution.py:221
  92.6 2.9 %multiply_subtract_fusion = f32[2,8,16,1280]{3,2,1,0:T(8,128)} fusion(f32[2,8,16,1280]{3,2,1,0:T(8,128)} %param.9, f32[2,8,16,1280]{3,2,1,0:T(8,128)} %bitcast.66, f32[]{:T(128)} %bitcast.20), kind=kLoop, calls=%fused_computation.8 | loop fusion | flops 655360 | bytes 3932164 | tf_op jit(solution)/shard_map/sub | solution.py:225
  (61 shorter events, 9.5 us)
Async XLA Ops:
  1.3 19.9 %collective-permute-start = (f32[2,4,256]{2,1,0:T(4,128)S(1)}, f32[2,4,256]{2,1,0:T(4,128)S(1)}, u32[]{:S(2)}, u32[]{:S(2)}) collective-permute-start(f32[2,4,256]{2,1,0:T(4,128)S(1)} %slice.76), channel_id=1, source_target_pairs={{0,128},{2,130},{4,132},{6,134},{8,136},{10,138},{12,140},{14,142}... | collective-permute-start | bytes 24584 | tf_op jit(solution)/shard_map/ppermute | solution.py:28
  15.8 5.3 %copy-start.4 = (s32[256]{0:T(256)S(1)}, s32[256]{0:T(256)}, u32[]{:S(2)}) copy-start(s32[256]{0:T(256)} %param.6) | copy-start | bytes 3076
  15.8 5.8 %copy-start.3 = (f32[2,4,4352]{2,1,0:T(4,128)S(1)}, f32[2,4,4352]{2,1,0:T(4,128)}, u32[]{:S(2)}) copy-start(f32[2,4,4352]{2,1,0:T(4,128)} %param.5) | copy-start | bytes 417796
  15.8 5.8 %slice-start = ((f32[2,4,4352]{2,1,0:T(4,128)}), f32[2,4,3840]{2,1,0:T(4,128)S(1)}, s32[]{:S(2)}) async-start(f32[2,4,4352]{2,1,0:T(4,128)} %param.5), calls=%async_computation.2 | async-start | bytes 245760 | tf_op jit(solution)/shard_map/slice | solution.py:55
  37.5 25.4 %all-to-all-start = ((f32[256,1,256]{2,1,0:T(1,128)}), f32[256,1,256]{2,1,0:T(1,128)S(1)}, u32[]{:S(2)}, u32[]{:S(2)}) async-start(f32[256,1,256]{2,1,0:T(1,128)} %all_to_all.19), calls=%async_computation | async-start | bytes 524288 | tf_op jit(solution)/shard_map/all_to_all | solution.py:124
  47.9 2.2 %copy-start = (f32[2,8,16,1280]{3,2,1,0:T(8,128)S(1)}, f32[2,8,16,1280]{3,2,1,0:T(8,128)}, u32[]{:S(2)}) copy-start(f32[2,8,16,1280]{3,2,1,0:T(8,128)} %param.9) | copy-start | bytes 3932164
  65.2 0.9 copy-start.1
  66.1 10.7 %copy-start.2 = (f32[256,128]{0,1:T(8,128)S(1)}, f32[256,128]{0,1:T(8,128)}, u32[]{:S(2)}) copy-start(f32[256,128]{0,1:T(8,128)} %get-tuple-element.15) | copy-start | bytes 393220
  70.6 19.2 %all-to-all-start.1 = ((f32[256,1,10]{2,1,0:T(1,128)}), f32[256,1,10]{2,1,0:T(1,128)S(1)}, u32[]{:S(2)}, u32[]{:S(2)}) async-start(f32[256,1,10]{2,1,0:T(1,128)} %bitcast.19), calls=%async_computation.1 | async-start | bytes 262144 | tf_op jit(solution)/shard_map/all_to_all | solution.py:221

commit v4 on v2

--- a/solution.py
+++ b/solution.py
@@ -110,7 +110,10 @@
     across_dev = (ang_index + ang_count // 2) % ang_count
     partner_slots = own_partners - across_dev * per_dev
     arrived = from_behind(projections[:, :, HALF:], ANG, ang_count // 2)
-    mirrored = jnp.flip(jnp.take(arrived, partner_slots, axis=0), axis=2)
+    chosen = arrived[0]
+    for slot in range(1, per_dev):
+        chosen = jnp.where((partner_slots == slot)[:, None, None], arrived[slot], chosen)
+    mirrored = jnp.flip(chosen, axis=2)
     stitched = blend_band(projections, mirrored, offsets)
     spec_real, spec_imag = spectrum_of(stitched)
     spectra = jnp.stack([spec_real, spec_imag])

time: 92.5 us -> 91.2 us (0.986)
  no operation moved by 1% of the time
where the time goes in v4:
time: 91.2 us; the launch traced here: 90.8 us
  blocking collectives  19 us (21%)
  starting transfers between devices  17.6 us (19%)
  other arithmetic  15.4 us (17%)
  matrix products  14.3 us (16%)
  local copies, waits for them, and re-layouts  11.9 us (13%)
  waiting for transfers between devices  10.3 us (11%)
  between operations  2.34 us (3%)
    all_to_all x1, blocking collectives, step_body(): received = lax.all_to_all(payload, ANG_SL, 0, 0, tiled=True)  19 us
    all_to_all x1, waiting for transfers between devices, step_body(): received = lax.all_to_all(payload, ANG_SL, 0, 0, tiled=True)  10.3 us
    all_to_all x1, starting transfers between devices, step_body(): received = lax.all_to_all(payload, ANG_SL, 0, 0, tiled=True)  9.84 us
    ppermute x1, starting transfers between devices, from_behind(): return lax.ppermute(value, axis, pairs)  7.73 us
    mul x1, other arithmetic, step_body(): jnp.cos(phase_tab) * norm_scale  5.36 us
    dot_general x1, matrix products, step_body(): lax.dot_general(tabs, tabs, (((1,), (1,)), ((), ())), precision=highest)  5.28 us
    transpose x1, local copies, waits for them, and re-layouts, step_body(): payload = spectra.transpose(2, 3, 0, 1, 4).reshape(dev_count, -1)  3.99 us
    all_to_all x1, local copies, waits for them, and re-layouts, step_body(): received = lax.all_to_all(payload, ANG_SL, 0, 0, tiled=True)  3.06 us
  transfers between devices with their start and end apart: 2, of which 1 were waited for; matrix products, arithmetic and copies ran while one was open for 20% of the time, Pallas kernels for 0%

profile of v4, /device:TPU:1, one launch (start us, length us, event | category | flops | bytes accessed | tf_op | source)
XLA Modules:
  0.0 90.8 jit_solution(10573149580300213394)
XLA Ops:
  0.6 0.7 slice.76
  1.3 7.7 %collective-permute-start = (f32[2,4,256]{2,1,0:T(4,128)S(1)}, f32[2,4,256]{2,1,0:T(4,128)S(1)}, u32[]{:S(2)}, u32[]{:S(2)}) collective-permute-start(f32[2,4,256]{2,1,0:T(4,128)S(1)} %slice.76), channel_id=1, source_target_pairs={{0,128},{2,130},{4,132},{6,134},{8,136},{10,138},{12,140},{14,142}... | collective-permute-start | bytes 24584 | tf_op jit(solution)/shard_map/ppermute | solution.py:28
  9.3 0.7 convert_element_type.76
  10.4 0.8 multiply_bitcast_fusion
  11.2 5.4 %fusion.3 = (f32[256,1280]{1,0:T(8,128)S(1)}, f32[256,1280]{1,0:T(8,128)S(1)}) fusion(f32[1280]{0:T(1024)S(1)} %add_convert_fusion, f32[256]{0:T(256)} %param.8), kind=kLoop, calls=%fused_computation.6 | loop fusion | flops 983040 | bytes 2627584 | tf_op jit(solution)/shard_map/mul | solution.py:165
  16.6 5.3 %fusion.1 = f32[512,512]{0,1:T(8,128)} fusion(f32[256,1280]{1,0:T(8,128)S(1)} %get-tuple-element.9, f32[256,1280]{1,0:T(8,128)S(1)} %get-tuple-element.8), kind=kOutput, calls=%fused_computation.4 | convolution fusion | flops 4027187200 | bytes 3670016 | tf_op jit(solution)/shard_map/dot_general | solution.py:192
  22.7 0.6 convolution_negate_fusion
  23.3 0.6 fusion.61
  25.1 1.0 %copy.37 = f32[8,32,128]{1,2,0:T(8,128)} copy(f32[8,32,128]{2,1,0:T(8,128)S(1)} %fusion.5) | data formatting | bytes 262144 | tf_op jit(solution)/shard_map/sub | solution.py:92
  26.7 2.1 %maximum_bitcast_fusion = f32[32,8,2,8,16]{0,4,1,3,2:T(8,128)} fusion(f32[1,8,32,8,16]{2,4,3,1,0:T(8,128)} %bitcast.68, f32[1,8,32,8,16]{2,4,3,1,0:T(8,128)S(1)} %bitcast.69), kind=kLoop, calls=%fused_computation.18 | loop fusion | flops 65536 | bytes 524288 | tf_op jit(solution)/shard_map/transpose | solution.py:123
  28.8 4.0 %copy.38 = f32[32,8,2,8,16]{4,3,2,1,0:T(8,128)} copy(f32[32,8,2,8,16]{0,4,1,3,2:T(8,128)} %maximum_bitcast_fusion) | data formatting | bytes 524288 | tf_op jit(solution)/shard_map/transpose | solution.py:123
  32.8 3.1 %all_to_all.19 = f32[256,1,256]{2,1,0:T(1,128)} reshape(f32[32,8,2,8,16]{4,3,2,1,0:T(8,128)} %copy.38) | data formatting | bytes 524288 | tf_op jit(solution)/shard_map/all_to_all | solution.py:124
  35.8 9.8 %all-to-all-start = ((f32[256,1,256]{2,1,0:T(1,128)}), f32[256,1,256]{2,1,0:T(1,128)S(1)}, u32[]{:S(2)}, u32[]{:S(2)}) async-start(f32[256,1,256]{2,1,0:T(1,128)} %all_to_all.19), calls=%async_computation | async-start | bytes 524288 | tf_op jit(solution)/shard_map/all_to_all | solution.py:124
  46.2 2.2 %fusion.157 = (f32[256,256]{0,1:T(8,128)}, f32[256,256]{0,1:T(8,128)}, f32[256,256]{0,1:T(8,128)}) fusion(f32[512,512]{0,1:T(8,128)} %fusion.1), kind=kLoop, calls=%fused_computation.219 | loop fusion | flops 196608 | bytes 1835008 | tf_op jit(solution)/shard_map/neg | solution.py:197
  48.4 2.5 %fusion.2 = f32[512,256]{0,1:T(8,128)S(1)} fusion(f32[256,1280]{1,0:T(8,128)S(1)} %bitcast.67, f32[256,1280]{1,0:T(8,128)S(1)} %get-tuple-element.9, f32[256,1280]{1,0:T(8,128)S(1)} %get-tuple-element.8), kind=kOutput, calls=%fused_computation.5 | convolution fusion | flops 2013921280 | bytes 4456448 | tf_op jit(solution)/shard_map/dot_general | solution.py:169
  50.9 10.3 %all-to-all-done = f32[256,1,256]{2,1,0:T(1,128)S(1)} async-done(((f32[256,1,256]{2,1,0:T(1,128)}), f32[256,1,256]{2,1,0:T(1,128)S(1)}, u32[]{:S(2)}, u32[]{:S(2)}) %all-to-all-start) | async-done | bytes 262176 | tf_op jit(solution)/shard_map/all_to_all | solution.py:124
  63.1 0.4 fusion.8
  63.5 0.8 add_reduce_fusion
  65.0 1.3 %pad_maximum_fusion.6 = f32[10]{0:T(128)S(1)} fusion(f32[1]{0:T(128)} %bitcast.19, f32[1]{0:T(128)} %bitcast.18), kind=kLoop, calls=%fused_computation.174 | loop fusion | flops 10 | bytes 48 | tf_op jit(solution)/shard_map/stack | solution.py:208
  66.4 19.0 %all_to_all.22 = f32[256,1,10]{2,1,0:T(1,128)S(1)} all-to-all(f32[256,1,10]{2,1,0:T(1,128)S(1)} %bitcast.71), channel_id=1, replica_groups=mesh['ang_0'=8,'ang_1'=2,'ang_2'=4,'ang_3'=2,'sl'=2] {'ang_0','ang_1','a..., dimensions={0} | all-to-all | bytes 20480 | tf_op jit(solution)/shard_map/all_to_all | solution.py:210
  85.6 0.7 fusion.158
  87.6 1.4 %fusion = f32[256,1280]{1,0:T(8,128)S(1)} fusion(f32[256,1280]{1,0:T(8,128)S(1)} %get-tuple-element.9, f32[256,1280]{1,0:T(8,128)S(1)} %get-tuple-element.8, f32[256,128]{0,1:T(8,128)S(1)} %get-tuple-element.7, f32[256,128]{0,1:T(8,128)S(1)} %copy-done.6, f32[256,128]{0,1:T(8,128)S(1)} %copy-done.4, f32[]{:T(128)} %bitcast.22), kind=kOutput, calls=%fused_computation.3 | convolution fusion | flops 1007812608 | bytes 4325380 | tf_op jit(solution)/shard_map/dot_general | solution.py:214
  89.0 1.2 %add.210 = f32[2,8,16,1280]{3,2,1,0:T(8,128)} add(f32[2,8,16,1280]{3,2,1,0:T(8,128)S(1)} %copy-done.1, f32[2,8,16,1280]{3,2,1,0:T(8,128)S(1)} %bitcast.66) | non-fusion elementwise | flops 327680 | bytes 3932160 | tf_op jit(solution)/shard_map/add | solution.py:217
  90.1 0.6 reshape.263
  (73 shorter events, 6.3 us)
Async XLA Ops:
  1.3 20.7 %collective-permute-start = (f32[2,4,256]{2,1,0:T(4,128)S(1)}, f32[2,4,256]{2,1,0:T(4,128)S(1)}, u32[]{:S(2)}, u32[]{:S(2)}) collective-permute-start(f32[2,4,256]{2,1,0:T(4,128)S(1)} %slice.76), channel_id=1, source_target_pairs={{0,128},{2,130},{4,132},{6,134},{8,136},{10,138},{12,140},{14,142}... | collective-permute-start | bytes 24584 | tf_op jit(solution)/shard_map/ppermute | solution.py:28
  16.6 5.3 %copy-start.11 = (s32[256]{0:T(256)S(1)}, s32[256]{0:T(256)}, u32[]{:S(2)}) copy-start(s32[256]{0:T(256)} %param.6) | copy-start | bytes 3076
  16.6 5.8 %copy-start.7 = (f32[2,4,4352]{2,1,0:T(4,128)S(1)}, f32[2,4,4352]{2,1,0:T(4,128)}, u32[]{:S(2)}) copy-start(f32[2,4,4352]{2,1,0:T(4,128)} %param.5) | copy-start | bytes 417796
  16.6 5.8 %slice-start = ((f32[2,4,4352]{2,1,0:T(4,128)}), f32[2,4,3840]{2,1,0:T(4,128)S(1)}, s32[]{:S(2)}) async-start(f32[2,4,4352]{2,1,0:T(4,128)} %param.5), calls=%async_computation.2 | async-start | bytes 245760 | tf_op jit(solution)/shard_map/slice | solution.py:55
  32.8 13.0 %copy-start.2 = (f32[8,16,8,16]{3,2,1,0:T(8,128)S(1)}, f32[8,16,8,16]{3,2,1,0:T(8,128)}, u32[]{:S(2)}) copy-start(f32[8,16,8,16]{3,2,1,0:T(8,128)} %multiply_bitcast_fusion) | copy-start | bytes 196612
  35.8 25.4 %all-to-all-start = ((f32[256,1,256]{2,1,0:T(1,128)}), f32[256,1,256]{2,1,0:T(1,128)S(1)}, u32[]{:S(2)}, u32[]{:S(2)}) async-start(f32[256,1,256]{2,1,0:T(1,128)} %all_to_all.19), calls=%async_computation | async-start | bytes 524288 | tf_op jit(solution)/shard_map/all_to_all | solution.py:124
  46.2 2.2 %copy-start = (f32[2,8,16,1280]{3,2,1,0:T(8,128)S(1)}, f32[2,8,16,1280]{3,2,1,0:T(8,128)}, u32[]{:S(2)}) copy-start(f32[2,8,16,1280]{3,2,1,0:T(8,128)} %param.9) | copy-start | bytes 3932164
  61.9 1.2 %copy-start.8 = (f32[256,256]{0,1:T(8,128)S(1)}, f32[256,256]{0,1:T(8,128)}, u32[]{:S(2)}) copy-start(f32[256,256]{0,1:T(8,128)} %get-tuple-element.4) | copy-start | bytes 786436
  61.9 1.2 %copy-start.9 = (f32[256,256]{0,1:T(8,128)S(1)}, f32[256,256]{0,1:T(8,128)}, u32[]{:S(2)}) copy-start(f32[256,256]{0,1:T(8,128)} %get-tuple-element.5) | copy-start | bytes 786436
  61.9 1.2 %copy-start.10 = (f32[256,256]{0,1:T(8,128)S(1)}, f32[256,256]{0,1:T(8,128)}, u32[]{:S(2)}) copy-start(f32[256,256]{0,1:T(8,128)} %get-tuple-element.6) | copy-start | bytes 786436
  62.9 1.4 %copy-start.3 = (f32[256,128]{0,1:T(8,128)}, f32[256,128]{0,1:T(8,128)S(1)}, u32[]{:S(2)}) copy-start(f32[256,128]{0,1:T(8,128)S(1)} %get-tuple-element.14) | copy-start | bytes 393220
  62.9 1.4 %copy-start.5 = (f32[256,128]{0,1:T(8,128)}, f32[256,128]{0,1:T(8,128)S(1)}, u32[]{:S(2)}) copy-start(f32[256,128]{0,1:T(8,128)S(1)} %get-tuple-element.15) | copy-start | bytes 393220
  64.3 23.2 %copy-start.4 = (f32[256,128]{0,1:T(8,128)S(1)}, f32[256,128]{0,1:T(8,128)}, u32[]{:S(2)}) copy-start(f32[256,128]{0,1:T(8,128)} %copy-done.3) | copy-start | bytes 393220
  64.3 23.2 %copy-start.6 = (f32[256,128]{0,1:T(8,128)S(1)}, f32[256,128]{0,1:T(8,128)}, u32[]{:S(2)}) copy-start(f32[256,128]{0,1:T(8,128)} %copy-done.5) | copy-start | bytes 393220
  87.6 1.4 %copy-start.1 = (f32[2,8,16,1280]{3,2,1,0:T(8,128)S(1)}, f32[2,8,16,1280]{3,2,1,0:T(8,128)}, u32[]{:S(2)}) copy-start(f32[2,8,16,1280]{3,2,1,0:T(8,128)} %param.9) | copy-start | bytes 3932164

commit v5 on v4

--- a/solution.py
+++ b/solution.py
@@ -109,7 +109,7 @@
     own_partners = lax.dynamic_slice_in_dim(partner, ang_index * per_dev, per_dev)
     across_dev = (ang_index + ang_count // 2) % ang_count
     partner_slots = own_partners - across_dev * per_dev
-    arrived = from_behind(projections[:, :, HALF:], ANG, ang_count // 2)
+    arrived = from_behind(projections, ANG, ang_count // 2)[:, :, HALF:]
     chosen = arrived[0]
     for slot in range(1, per_dev):
         chosen = jnp.where((partner_slots == slot)[:, None, None], arrived[slot], chosen)
@@ -201,11 +201,42 @@
     resid_both = jnp.concatenate([resid_real, resid_imag])
     image_both = jnp.dot(gram_both, resid_both, precision=lax.Precision.HIGH)
     image_real, image_imag = image_both[:total_angles], image_both[total_angles:]
-    curvature = jnp.sum(ramp_weights * (image_real * image_real + image_imag * image_imag))
-    grad_norm = jnp.sum(resid_real * image_real + resid_imag * image_imag)
-    by_owner = misfit_table.reshape(ang_count, per_dev, sl_count, rows_dev)
-    by_owner = jnp.swapaxes(by_owner, 1, 2).reshape(ang_count * sl_count, per_dev * rows_dev)
-    scalars = jnp.broadcast_to(jnp.stack([grad_norm, curvature])[None], (ang_count * sl_count, 2))
+    owners = ang_count * sl_count
+    if per_dev == 2 and sl_count == 2:
+        cells = jnp.concatenate(
+            [
+                diff_real * resid_real + diff_imag * resid_imag,
+                resid_real * image_real + resid_imag * image_imag,
+                ramp_weights * (image_real * image_real + image_imag * image_imag),
+            ],
+            axis=1,
+        )
+        cell_ids = jnp.arange(3 * columns, dtype=jnp.int32)
+        out_ids = jnp.arange(ROWS + 2, dtype=jnp.int32)
+        target = jnp.where(
+            cell_ids < columns, cell_ids // block_freqs, ROWS + cell_ids // columns - 1
+        )
+        scale = jnp.where(cell_ids < columns, 1.0 / K, 1.0).astype(jnp.float32)
+        summing = jnp.where(target[:, None] == out_ids[None, :], scale[:, None], 0.0)
+        sums = jnp.dot(cells, summing, precision=highest)
+        table = sums[:, :ROWS]
+        row_ids = jnp.arange(owners, dtype=jnp.int32)
+        lane_ids = jnp.arange(ROWS, dtype=jnp.int32)
+        row_swap = ((row_ids[:, None] ^ 1) == row_ids[None, :]).astype(jnp.float32)
+        lane_swap = ((lane_ids[:, None] ^ rows_dev) == lane_ids[None, :]).astype(jnp.float32)
+        swapped = jnp.dot(
+            row_swap, jnp.dot(table, lane_swap, precision=highest), precision=highest
+        )
+        same_half = (row_ids[:, None] % 2) == ((lane_ids[None, :] // rows_dev) % 2)
+        by_owner = jnp.where(same_half, table, swapped)
+        spread = jnp.ones((owners, total_angles), jnp.float32)
+        scalars = jnp.dot(spread, sums[:, ROWS:], precision=highest)
+    else:
+        curvature = jnp.sum(ramp_weights * (image_real * image_real + image_imag * image_imag))
+        grad_norm = jnp.sum(resid_real * image_real + resid_imag * image_imag)
+        by_owner = misfit_table.reshape(ang_count, per_dev, sl_count, rows_dev)
+        by_owner = jnp.swapaxes(by_owner, 1, 2).reshape(owners, per_dev * rows_dev)
+        scalars = jnp.broadcast_to(jnp.stack([grad_norm, curvature])[None], (owners, 2))
     payload = jnp.concatenate([by_owner, scalars], axis=1)
     received = lax.all_to_all(payload, ANG_SL, 0, 0, tiled=True)
     totals = jnp.sum(received, axis=0)

time: 91.2 us -> 89.6 us (0.982)
  other arithmetic: 15.4 us -> 13.5 us
  matrix products: 14.3 us -> 15.4 us
  local copies, waits for them, and re-layouts: 11.9 us -> 10.9 us
    another operation x2, other arithmetic: 1.34 us -> 0.12 us  [the longest x1 1.34 us: step_body(): jnp.stack([grad_norm, curvature])[None]]
    dot_general x0 -> x3, matrix products: none -> 1.11 us  [the longest x1 0.59 us: step_body(): sums = jnp.dot(cells, summing, precision=highest)]
    all_to_all x1 -> x2, local copies, waits for them, and re-layouts: 3.06 us -> 3.18 us  [step_body(): received = lax.all_to_all(payload, ANG_SL, 0, 0, tiled=True)]
where the time goes in v5:
time: 89.6 us; the launch traced here: 89.2 us
  blocking collectives  19 us (21%)
  starting transfers between devices  17.7 us (20%)
  matrix products  15.4 us (17%)
  other arithmetic  13.5 us (15%)
  local copies, waits for them, and re-layouts  10.9 us (12%)
  waiting for transfers between devices  10.3 us (11%)
  between operations  2.38 us (3%)
    all_to_all x1, blocking collectives, step_body(): received = lax.all_to_all(payload, ANG_SL, 0, 0, tiled=True)  19 us
    all_to_all x1, waiting for transfers between devices, step_body(): received = lax.all_to_all(payload, ANG_SL, 0, 0, tiled=True)  10.3 us
    all_to_all x1, starting transfers between devices, step_body(): received = lax.all_to_all(payload, ANG_SL, 0, 0, tiled=True)  9.85 us
    ppermute x1, starting transfers between devices, from_behind(): return lax.ppermute(value, axis, pairs)  7.81 us
    mul x1, other arithmetic, step_body(): jnp.cos(phase_tab) * norm_scale  5.4 us
    dot_general x1, matrix products, step_body(): lax.dot_general(tabs, tabs, (((1,), (1,)), ((), ())), precision=highest)  5.27 us
    transpose x1, local copies, waits for them, and re-layouts, step_body(): payload = spectra.transpose(2, 3, 0, 1, 4).reshape(dev_count, -1)  4 us
    all_to_all x2, local copies, waits for them, and re-layouts, step_body(): received = lax.all_to_all(payload, ANG_SL, 0, 0, tiled=True)  3.18 us
  transfers between devices with their start and end apart: 2, of which 1 were waited for; matrix products, arithmetic and copies ran while one was open for 20% of the time, Pallas kernels for 0%

profile of v5, /device:TPU:1, one launch (start us, length us, event | category | flops | bytes accessed | tf_op | source)
XLA Modules:
  0.0 89.2 jit_solution(279359214293433551)
XLA Ops:
  0.6 7.8 %collective-permute-start = (f32[2,4,4352]{2,1,0:T(4,128)}, f32[2,4,4352]{2,1,0:T(4,128)S(1)}, u32[]{:S(2)}, u32[]{:S(2)}) collective-permute-start(f32[2,4,4352]{2,1,0:T(4,128)} %param.5), channel_id=1, source_target_pairs={{0,128},{2,130},{4,132},{6,134},{8,136},{10,138},{12,140},{14,142}... | collective-permute-start | bytes 417800 | tf_op jit(solution)/shard_map/ppermute | solution.py:28
  8.8 0.7 convert_element_type.78
  9.9 0.8 multiply_bitcast_fusion
  10.7 5.4 %fusion.3 = (f32[256,1280]{1,0:T(8,128)S(1)}, f32[256,1280]{1,0:T(8,128)S(1)}) fusion(f32[1280]{0:T(1024)S(1)} %add_convert_fusion, f32[256]{0:T(256)} %param.8), kind=kLoop, calls=%fused_computation.6 | loop fusion | flops 983040 | bytes 2627584 | tf_op jit(solution)/shard_map/mul | solution.py:165
  16.2 5.3 %fusion.1 = f32[512,512]{0,1:T(8,128)} fusion(f32[256,1280]{1,0:T(8,128)S(1)} %get-tuple-element.12, f32[256,1280]{1,0:T(8,128)S(1)} %get-tuple-element.11), kind=kOutput, calls=%fused_computation.4 | convolution fusion | flops 4027187200 | bytes 3670016 | tf_op jit(solution)/shard_map/dot_general | solution.py:192
  22.1 0.6 convolution_negate_fusion
  22.8 0.6 fusion.72
  24.2 0.4 fusion.6
  24.6 1.0 %copy.18 = f32[8,32,128]{1,2,0:T(8,128)} copy(f32[8,32,128]{2,1,0:T(8,128)S(1)} %fusion.6) | data formatting | bytes 262144 | tf_op jit(solution)/shard_map/add | solution.py:89
  25.6 0.4 fusion.5
  26.2 2.1 %maximum_bitcast_fusion = f32[32,8,2,8,16]{0,4,1,3,2:T(8,128)} fusion(f32[1,8,32,8,16]{2,4,3,1,0:T(8,128)S(1)} %bitcast.64, f32[1,8,32,8,16]{2,4,3,1,0:T(8,128)} %bitcast.63), kind=kLoop, calls=%fused_computation.19 | loop fusion | flops 65536 | bytes 524288 | tf_op jit(solution)/shard_map/transpose | solution.py:123
  28.3 4.0 %copy.20 = f32[32,8,2,8,16]{4,3,2,1,0:T(8,128)} copy(f32[32,8,2,8,16]{0,4,1,3,2:T(8,128)} %maximum_bitcast_fusion) | data formatting | bytes 524288 | tf_op jit(solution)/shard_map/transpose | solution.py:123
  32.3 3.1 %all_to_all.19 = f32[256,1,256]{2,1,0:T(1,128)} reshape(f32[32,8,2,8,16]{4,3,2,1,0:T(8,128)} %copy.20) | data formatting | bytes 524288 | tf_op jit(solution)/shard_map/all_to_all | solution.py:124
  35.4 9.9 %all-to-all-start = ((f32[256,1,256]{2,1,0:T(1,128)}), f32[256,1,256]{2,1,0:T(1,128)S(1)}, u32[]{:S(2)}, u32[]{:S(2)}) async-start(f32[256,1,256]{2,1,0:T(1,128)} %all_to_all.19), calls=%async_computation | async-start | bytes 524288 | tf_op jit(solution)/shard_map/all_to_all | solution.py:124
  45.7 2.2 %fusion.182 = (f32[256,256]{0,1:T(8,128)}, f32[256,256]{0,1:T(8,128)}, f32[256,256]{0,1:T(8,128)}) fusion(f32[512,512]{0,1:T(8,128)} %fusion.1), kind=kLoop, calls=%fused_computation.261 | loop fusion | flops 196608 | bytes 1835008 | tf_op jit(solution)/shard_map/neg | solution.py:197
  47.9 2.5 %fusion.2 = f32[512,256]{0,1:T(8,128)S(1)} fusion(f32[256,1280]{1,0:T(8,128)S(1)} %bitcast.62, f32[256,1280]{1,0:T(8,128)S(1)} %get-tuple-element.12, f32[256,1280]{1,0:T(8,128)S(1)} %get-tuple-element.11), kind=kOutput, calls=%fused_computation.5 | convolution fusion | flops 2013921280 | bytes 4456448 | tf_op jit(solution)/shard_map/dot_general | solution.py:169
  50.4 10.3 %all-to-all-done = f32[256,1,256]{2,1,0:T(1,128)S(1)} async-done(((f32[256,1,256]{2,1,0:T(1,128)}), f32[256,1,256]{2,1,0:T(1,128)S(1)}, u32[]{:S(2)}, u32[]{:S(2)}) %all-to-all-start) | async-done | bytes 262176 | tf_op jit(solution)/shard_map/all_to_all | solution.py:124
  62.5 0.4 fusion.8
  63.1 0.6 fusion.22
  64.7 19.0 %all_to_all.22 = f32[256,1,10]{2,1,0:T(1,128)S(1)} all-to-all(f32[256,1,10]{2,1,0:T(1,128)S(1)} %copy.23), channel_id=1, replica_groups=mesh['ang_0'=8,'ang_1'=2,'ang_2'=4,'ang_3'=2,'sl'=2] {'ang_0','ang_1','a..., dimensions={0} | all-to-all | bytes 20480 | tf_op jit(solution)/shard_map/all_to_all | solution.py:241
  84.0 0.7 fusion.183
  86.0 1.4 %fusion = f32[256,1280]{1,0:T(8,128)S(1)} fusion(f32[256,1280]{1,0:T(8,128)S(1)} %get-tuple-element.12, f32[256,1280]{1,0:T(8,128)S(1)} %get-tuple-element.11, f32[256,128]{0,1:T(8,128)S(1)} %get-tuple-element.10, f32[256,128]{0,1:T(8,128)S(1)} %copy-done.6, f32[256,128]{0,1:T(8,128)S(1)} %copy-done.4, f32[]{:T(128)} %bitcast.17), kind=kOutput, calls=%fused_computation.3 | convolution fusion | flops 1007812608 | bytes 4325380 | tf_op jit(solution)/shard_map/dot_general | solution.py:245
  87.4 1.2 %add.254 = f32[2,8,16,1280]{3,2,1,0:T(8,128)} add(f32[2,8,16,1280]{3,2,1,0:T(8,128)S(1)} %copy-done.1, f32[2,8,16,1280]{3,2,1,0:T(8,128)S(1)} %bitcast.61) | non-fusion elementwise | flops 327680 | bytes 3932160 | tf_op jit(solution)/shard_map/add | solution.py:248
  88.6 0.6 reshape.337
  (74 shorter events, 5.9 us)
Async XLA Ops:
  0.6 20.9 %collective-permute-start = (f32[2,4,4352]{2,1,0:T(4,128)}, f32[2,4,4352]{2,1,0:T(4,128)S(1)}, u32[]{:S(2)}, u32[]{:S(2)}) collective-permute-start(f32[2,4,4352]{2,1,0:T(4,128)} %param.5), channel_id=1, source_target_pairs={{0,128},{2,130},{4,132},{6,134},{8,136},{10,138},{12,140},{14,142}... | collective-permute-start | bytes 417800 | tf_op jit(solution)/shard_map/ppermute | solution.py:28
  10.7 5.4 %copy-start.11 = (s32[256]{0:T(256)S(1)}, s32[256]{0:T(256)}, u32[]{:S(2)}) copy-start(s32[256]{0:T(256)} %param.6) | copy-start | bytes 3076
  10.7 5.5 %copy-start.10 = (f32[2,4,4352]{2,1,0:T(4,128)S(1)}, f32[2,4,4352]{2,1,0:T(4,128)}, u32[]{:S(2)}) copy-start(f32[2,4,4352]{2,1,0:T(4,128)} %param.5) | copy-start | bytes 417796
  32.3 12.9 %copy-start.2 = (f32[8,16,8,16]{3,2,1,0:T(8,128)S(1)}, f32[8,16,8,16]{3,2,1,0:T(8,128)}, u32[]{:S(2)}) copy-start(f32[8,16,8,16]{3,2,1,0:T(8,128)} %multiply_bitcast_fusion) | copy-start | bytes 196612
  35.4 25.4 %all-to-all-start = ((f32[256,1,256]{2,1,0:T(1,128)}), f32[256,1,256]{2,1,0:T(1,128)S(1)}, u32[]{:S(2)}, u32[]{:S(2)}) async-start(f32[256,1,256]{2,1,0:T(1,128)} %all_to_all.19), calls=%async_computation | async-start | bytes 524288 | tf_op jit(solution)/shard_map/all_to_all | solution.py:124
  45.7 2.2 %copy-start = (f32[2,8,16,1280]{3,2,1,0:T(8,128)S(1)}, f32[2,8,16,1280]{3,2,1,0:T(8,128)}, u32[]{:S(2)}) copy-start(f32[2,8,16,1280]{3,2,1,0:T(8,128)} %param.9) | copy-start | bytes 3932164
  61.1 1.4 %copy-start.7 = (f32[256,256]{0,1:T(8,128)S(1)}, f32[256,256]{0,1:T(8,128)}, u32[]{:S(2)}) copy-start(f32[256,256]{0,1:T(8,128)} %get-tuple-element.2) | copy-start | bytes 786436
  61.1 1.4 %copy-start.8 = (f32[256,256]{0,1:T(8,128)S(1)}, f32[256,256]{0,1:T(8,128)}, u32[]{:S(2)}) copy-start(f32[256,256]{0,1:T(8,128)} %get-tuple-element.3) | copy-start | bytes 786436
  61.1 1.4 %copy-start.9 = (f32[256,256]{0,1:T(8,128)S(1)}, f32[256,256]{0,1:T(8,128)}, u32[]{:S(2)}) copy-start(f32[256,256]{0,1:T(8,128)} %get-tuple-element.4) | copy-start | bytes 786436
  62.4 0.6 copy-start.3
  62.5 0.7 copy-start.5
  63.1 22.8 %copy-start.4 = (f32[256,128]{0,1:T(8,128)S(1)}, f32[256,128]{0,1:T(8,128)}, u32[]{:S(2)}) copy-start(f32[256,128]{0,1:T(8,128)} %copy-done.3) | copy-start | bytes 393220
  63.1 22.9 %copy-start.6 = (f32[256,128]{0,1:T(8,128)S(1)}, f32[256,128]{0,1:T(8,128)}, u32[]{:S(2)}) copy-start(f32[256,128]{0,1:T(8,128)} %copy-done.5) | copy-start | bytes 393220
  86.0 1.4 %copy-start.1 = (f32[2,8,16,1280]{3,2,1,0:T(8,128)S(1)}, f32[2,8,16,1280]{3,2,1,0:T(8,128)}, u32[]{:S(2)}) copy-start(f32[2,8,16,1280]{3,2,1,0:T(8,128)} %param.9) | copy-start | bytes 3932164

commit v6 on v5

--- a/solution.py
+++ b/solution.py
@@ -69,8 +69,9 @@
     )
     first_cos = jnp.cos(first_phase) * norm_scale
     first_sin = jnp.sin(first_phase) * norm_scale
-    part_real = jnp.einsum("rab,ap->rbp", folded, first_cos, precision=highest)
-    part_imag = -jnp.einsum("rab,ap->rbp", folded, first_sin, precision=highest)
+    first_both = jnp.concatenate([first_cos, -first_sin], axis=1)
+    part = jnp.einsum("rab,ap->rbp", folded, first_both, precision=highest)
+    part_real, part_imag = part[:, :, :128], part[:, :, 128:]
     low_ids = jnp.arange(low_split, dtype=jnp.int32)
     twist_phase = 2.0 * math.pi / W * (low_ids[:, None] * lane_ids[None, :]).astype(jnp.float32)
     twist_cos = jnp.cos(twist_phase)
@@ -86,12 +87,15 @@
     )
     last_cos = jnp.cos(last_phase)
     last_sin = jnp.sin(last_phase)
-    spec_real = jnp.einsum("rbp,bq->rqp", turned_real, last_cos, precision=highest) + jnp.einsum(
-        "rbp,bq->rqp", turned_imag, last_sin, precision=highest
-    )
-    spec_imag = jnp.einsum("rbp,bq->rqp", turned_imag, last_cos, precision=highest) - jnp.einsum(
-        "rbp,bq->rqp", turned_real, last_sin, precision=highest
-    )
+    turned = jnp.concatenate([turned_real, turned_imag], axis=1)
+    last_both = jnp.concatenate(
+        [
+            jnp.concatenate([last_cos, -last_sin], axis=1),
+            jnp.concatenate([last_sin, last_cos], axis=1),
+        ]
+    )
+    spec = jnp.einsum("rbp,bq->rqp", turned, last_both, precision=highest)
+    spec_real, spec_imag = spec[:, :high_count], spec[:, high_count:]
     return (spec_real, spec_imag)
 
 
@@ -109,7 +113,7 @@
     own_partners = lax.dynamic_slice_in_dim(partner, ang_index * per_dev, per_dev)
     across_dev = (ang_index + ang_count // 2) % ang_count
     partner_slots = own_partners - across_dev * per_dev
-    arrived = from_behind(projections, ANG, ang_count // 2)[:, :, HALF:]
+    arrived = from_behind(projections[:, :, HALF:], ANG, ang_count // 2)
     chosen = arrived[0]
     for slot in range(1, per_dev):
         chosen = jnp.where((partner_slots == slot)[:, None, None], arrived[slot], chosen)
@@ -245,7 +249,7 @@
     step_grad = lax.dot_general(
         -step_size * stacked, tabs, (((0,), (0,)), ((), ())), precision=lax.Precision.HIGH
     )
-    updated = coefficients + step_grad.reshape(coefficients.shape)
+    updated = (coef_rows + step_grad).reshape(coefficients.shape)
     return (updated, misfit)
 
 

time: 89.6 us -> 98.4 us (1.098)
  other arithmetic: 13.5 us -> 19.7 us
  local copies, waits for them, and re-layouts: 10.9 us -> 12.4 us
  matrix products: 15.4 us -> 16.8 us
    slice x0 -> x4, local copies, waits for them, and re-layouts: none -> 2.76 us  [the longest x3 2.06 us: spectrum_of(): spec_real, spec_imag = (spec[:, :high_count], spec[:, high_count:])]
    dot_general x1, matrix products: 1.35 us -> 3.69 us  [step_body(): lax.dot_general(-step_size * stacked, tabs, (((0,), (0,)), ((), ())), pre...]
    neg x0 -> x2, other arithmetic: none -> 1.46 us  [the longest x1 0.78 us: spectrum_of(): first_both = jnp.concatenate([first_cos, -first_sin], axis=1)]
    add x1 -> x0, local copies, waits for them, and re-layouts: 1.01 us -> none  [spectrum_of(): jnp.einsum('rbp,bq->rqp', turned_real, last_cos, precision=highest)]
    dot_general x6 -> x2, matrix products: 2.77 us -> 1.83 us  [the longest x1 1.4 us: spectrum_of(): part = jnp.einsum('rab,ap->rbp', folded, first_both, precision=highest)]
  transfers between devices with their start and end apart: 2 -> 2, of which waited for: 1 -> 1; matrix products, arithmetic and copies ran while one was open for 20% -> 25% of each run, Pallas kernels for 0% -> 0%
where the time goes in v6:
time: 98.4 us; the launch traced here: 97.9 us
  other arithmetic  19.7 us (20%)
  blocking collectives  18.7 us (19%)
  starting transfers between devices  17.6 us (18%)
  matrix products  16.8 us (17%)
  local copies, waits for them, and re-layouts  12.4 us (13%)
  waiting for transfers between devices  10.2 us (10%)
  between operations  2.34 us (2%)
    all_to_all x1, blocking collectives, step_body(): received = lax.all_to_all(payload, ANG_SL, 0, 0, tiled=True)  18.7 us
    all_to_all x1, waiting for transfers between devices, step_body(): received = lax.all_to_all(payload, ANG_SL, 0, 0, tiled=True)  10.2 us
    all_to_all x1, starting transfers between devices, step_body(): received = lax.all_to_all(payload, ANG_SL, 0, 0, tiled=True)  9.85 us
    ppermute x1, starting transfers between devices, from_behind(): return lax.ppermute(value, axis, pairs)  7.73 us
    mul x1, other arithmetic, step_body(): jnp.cos(phase_tab) * norm_scale  5.36 us
    dot_general x1, matrix products, step_body(): lax.dot_general(tabs, tabs, (((1,), (1,)), ((), ())), precision=highest)  5.3 us
    transpose x1, local copies, waits for them, and re-layouts, step_body(): payload = spectra.transpose(2, 3, 0, 1, 4).reshape(dev_count, -1)  4.02 us
    dot_general x1, matrix products, step_body(): lax.dot_general(-step_size * stacked, tabs, (((0,), (0,)), ((), ())), pre...  3.69 us
  transfers between devices with their start and end apart: 2, of which 1 were waited for; matrix products, arithmetic and copies ran while one was open for 25% of the time, Pallas kernels for 0%

profile of v6, /device:TPU:1, one launch (start us, length us, event | category | flops | bytes accessed | tf_op | source)
XLA Modules:
  0.0 97.9 jit_solution(12413813128526997578)
XLA Ops:
  0.6 0.7 slice.94
  1.3 7.7 %collective-permute-start = (f32[2,4,256]{2,1,0:T(4,128)S(1)}, f32[2,4,256]{2,1,0:T(4,128)S(1)}, u32[]{:S(2)}, u32[]{:S(2)}) collective-permute-start(f32[2,4,256]{2,1,0:T(4,128)S(1)} %slice.94), channel_id=1, source_target_pairs={{0,128},{2,130},{4,132},{6,134},{8,136},{10,138},{12,140},{14,142}... | collective-permute-start | bytes 24584 | tf_op jit(solution)/shard_map/ppermute | solution.py:28
  9.1 0.8 multiply_negate_fusion
  9.8 0.8 fusion.80
  10.6 0.7 fusion.99
  11.3 0.7 fusion.103
  14.3 0.6 fusion.130
  16.5 0.7 convert_element_type.78
  17.7 5.4 %fusion.2 = (f32[256,1280]{1,0:T(8,128)S(1)}, f32[256,1280]{1,0:T(8,128)S(1)}) fusion(f32[1280]{0:T(1024)S(1)} %add_convert_fusion, f32[256]{0:T(256)} %param.8), kind=kLoop, calls=%fused_computation.6 | loop fusion | flops 983040 | bytes 2627584 | tf_op jit(solution)/shard_map/mul | solution.py:169
  23.1 5.3 %fusion = f32[512,512]{0,1:T(8,128)} fusion(f32[256,1280]{1,0:T(8,128)S(1)} %get-tuple-element.14, f32[256,1280]{1,0:T(8,128)S(1)} %get-tuple-element.13), kind=kOutput, calls=%fused_computation.4 | convolution fusion | flops 4027187200 | bytes 3670016 | tf_op jit(solution)/shard_map/dot_general | solution.py:196
  29.1 1.4 %fusion.56 = f32[8,64,256]{2,1,0:T(8,128)S(1)} fusion(f32[8,64,64]{2,1,0:T(8,128)S(1)} %reshape.334, f32[64,128]{1,0:T(8,128)} %get-tuple-element.26, f32[64,128]{1,0:T(8,128)} %get-tuple-element.27), kind=kOutput, calls=%fused_computation.84 | convolution fusion | flops 100679680 | bytes 720896 | tf_op jit(solution)/shard_map/rab,ap->rbp/dot_general | solution.py:73
  30.5 0.8 multiply_add_fusion
  31.9 1.0 %copy.16 = f32[8,32,128]{1,2,0:T(8,128)} copy(f32[8,32,128]{2,1,0:T(8,128)S(1)} %get-tuple-element.10) | data formatting | bytes 262144 | tf_op jit(solution)/shard_map/slice | solution.py:98
  32.9 1.0 %copy.17 = f32[8,32,128]{1,2,0:T(8,128)} copy(f32[8,32,128]{2,1,0:T(8,128)S(1)} %get-tuple-element.11) | data formatting | bytes 262144 | tf_op jit(solution)/shard_map/slice | solution.py:98
  33.9 2.3 %maximum_bitcast_fusion = f32[32,8,2,8,16]{0,4,1,3,2:T(8,128)} fusion(f32[1,8,32,8,16]{2,4,3,1,0:T(8,128)} %bitcast.51, f32[1,8,32,8,16]{2,4,3,1,0:T(8,128)} %bitcast.50), kind=kLoop, calls=%fused_computation.15 | loop fusion | flops 65536 | bytes 524288 | tf_op jit(solution)/shard_map/transpose | solution.py:127
  36.2 4.0 %copy.18 = f32[32,8,2,8,16]{4,3,2,1,0:T(8,128)} copy(f32[32,8,2,8,16]{0,4,1,3,2:T(8,128)} %maximum_bitcast_fusion) | data formatting | bytes 524288 | tf_op jit(solution)/shard_map/transpose | solution.py:127
  40.2 3.0 %all_to_all.19 = f32[256,1,256]{2,1,0:T(1,128)} reshape(f32[32,8,2,8,16]{4,3,2,1,0:T(8,128)} %copy.18) | data formatting | bytes 524288 | tf_op jit(solution)/shard_map/all_to_all | solution.py:128
  43.2 9.9 %all-to-all-start = ((f32[256,1,256]{2,1,0:T(1,128)}), f32[256,1,256]{2,1,0:T(1,128)S(1)}, u32[]{:S(2)}, u32[]{:S(2)}) async-start(f32[256,1,256]{2,1,0:T(1,128)} %all_to_all.19), calls=%async_computation | async-start | bytes 524288 | tf_op jit(solution)/shard_map/all_to_all | solution.py:128
  53.6 2.3 %fusion.147 = (f32[256,256]{0,1:T(8,128)}, f32[256,256]{0,1:T(8,128)}, f32[256,256]{0,1:T(8,128)}) fusion(f32[512,512]{0,1:T(8,128)} %fusion), kind=kLoop, calls=%fused_computation.235 | loop fusion | flops 196608 | bytes 1835008 | tf_op jit(solution)/shard_map/neg | solution.py:201
  55.8 2.5 %fusion.1 = f32[512,256]{0,1:T(8,128)S(1)} fusion(f32[256,1280]{1,0:T(8,128)S(1)} %bitcast.49, f32[256,1280]{1,0:T(8,128)S(1)} %get-tuple-element.14, f32[256,1280]{1,0:T(8,128)S(1)} %get-tuple-element.13), kind=kOutput, calls=%fused_computation.5 | convolution fusion | flops 2013921280 | bytes 4456448 | tf_op jit(solution)/shard_map/dot_general | solution.py:173
  58.3 10.2 %all-to-all-done = f32[256,1,256]{2,1,0:T(1,128)S(1)} async-done(((f32[256,1,256]{2,1,0:T(1,128)}), f32[256,1,256]{2,1,0:T(1,128)S(1)}, u32[]{:S(2)}, u32[]{:S(2)}) %all-to-all-start) | async-done | bytes 262176 | tf_op jit(solution)/shard_map/all_to_all | solution.py:128
  72.6 18.7 %all_to_all.22 = f32[256,1,10]{2,1,0:T(1,128)S(1)} all-to-all(f32[256,1,10]{2,1,0:T(1,128)S(1)} %copy.21), channel_id=1, replica_groups=mesh['ang_0'=8,'ang_1'=2,'ang_2'=4,'ang_3'=2,'sl'=2] {'ang_0','ang_1','a..., dimensions={0} | all-to-all | bytes 20480 | tf_op jit(solution)/shard_map/all_to_all | solution.py:245
  93.6 0.6 reshape.337
  94.2 3.7 %convolution_add_fusion = f32[256,1280]{1,0:T(8,128)} fusion(f32[256,1280]{1,0:T(8,128)} %bitcast.48, f32[256,1280]{1,0:T(8,128)S(1)} %get-tuple-element.14, f32[256,1280]{1,0:T(8,128)S(1)} %get-tuple-element.13, f32[256,128]{0,1:T(8,128)S(1)} %get-tuple-element.12, f32[256,128]{0,1:T(8,128)S(1)} %get-tuple-element.20, f32[256,128]{0,1:T(8,128)S(1)} %get-tuple-element.19, ...), kind=kOutput, calls=%fused_computation | convolution fusion | flops 1008140288 | bytes 5636100 | tf_op jit(solution)/shard_map/dot_general | solution.py:249
  (90 shorter events, 10.8 us)
Async XLA Ops:
  1.3 27.1 %collective-permute-start = (f32[2,4,256]{2,1,0:T(4,128)S(1)}, f32[2,4,256]{2,1,0:T(4,128)S(1)}, u32[]{:S(2)}, u32[]{:S(2)}) collective-permute-start(f32[2,4,256]{2,1,0:T(4,128)S(1)} %slice.94), channel_id=1, source_target_pairs={{0,128},{2,130},{4,132},{6,134},{8,136},{10,138},{12,140},{14,142}... | collective-permute-start | bytes 24584 | tf_op jit(solution)/shard_map/ppermute | solution.py:28
  23.0 5.3 %copy-start.9 = (s32[256]{0:T(256)S(1)}, s32[256]{0:T(256)}, u32[]{:S(2)}) copy-start(s32[256]{0:T(256)} %param.6) | copy-start | bytes 3076
  23.1 5.8 %copy-start.1 = (f32[2,4,4352]{2,1,0:T(4,128)S(1)}, f32[2,4,4352]{2,1,0:T(4,128)}, u32[]{:S(2)}) copy-start(f32[2,4,4352]{2,1,0:T(4,128)} %param.5) | copy-start | bytes 417796
  23.1 5.8 %slice-start = ((f32[2,4,4352]{2,1,0:T(4,128)}), f32[2,4,3840]{2,1,0:T(4,128)S(1)}, s32[]{:S(2)}) async-start(f32[2,4,4352]{2,1,0:T(4,128)} %param.5), calls=%async_computation.2 | async-start | bytes 245760 | tf_op jit(solution)/shard_map/slice | solution.py:55
  29.1 2.3 %copy-start.5 = (f32[64,32]{0,1:T(8,128)S(1)}, f32[64,32]{0,1:T(8,128)}, u32[]{:S(2)}) copy-start(f32[64,32]{0,1:T(8,128)} %get-tuple-element.31) | copy-start | bytes 24580
  29.1 2.3 %copy-start.6 = (f32[64,32]{0,1:T(8,128)S(1)}, f32[64,32]{0,1:T(8,128)}, u32[]{:S(2)}) copy-start(f32[64,32]{0,1:T(8,128)} %fusion.103) | copy-start | bytes 24580
  40.2 13.1 %copy-start.17 = (f32[16]{0:T(128)S(1)}, f32[16]{0:T(128)}, u32[]{:S(2)}) copy-start(f32[16]{0:T(128)} %get-tuple-element.25) | copy-start | bytes 196
  40.2 13.2 %copy-start.16 = (f32[16]{0:T(128)S(1)}, f32[16]{0:T(128)}, u32[]{:S(2)}) copy-start(f32[16]{0:T(128)} %get-tuple-element.24) | copy-start | bytes 196
  40.2 13.3 %copy-start.15 = (f32[16]{0:T(128)S(1)}, f32[16]{0:T(128)}, u32[]{:S(2)}) copy-start(f32[16]{0:T(128)} %get-tuple-element.22) | copy-start | bytes 196
  43.2 25.4 %all-to-all-start = ((f32[256,1,256]{2,1,0:T(1,128)}), f32[256,1,256]{2,1,0:T(1,128)S(1)}, u32[]{:S(2)}, u32[]{:S(2)}) async-start(f32[256,1,256]{2,1,0:T(1,128)} %all_to_all.19), calls=%async_computation | async-start | bytes 524288 | tf_op jit(solution)/shard_map/all_to_all | solution.py:128
  53.6 2.3 %copy-start = (f32[2,8,16,1280]{3,2,1,0:T(8,128)S(1)}, f32[2,8,16,1280]{3,2,1,0:T(8,128)}, u32[]{:S(2)}) copy-start(f32[2,8,16,1280]{3,2,1,0:T(8,128)} %param.9) | copy-start | bytes 3932164
  55.8 12.8 %copy-start.14 = (s32[256]{0:T(256)S(1)}, s32[256]{0:T(256)}, u32[]{:S(2)}) copy-start(s32[256]{0:T(256)} %iota_xor_fusion) | copy-start | bytes 3076
  55.8 13.1 %copy-start.7 = (s32[256]{0:T(256)S(1)}, s32[256]{0:T(256)}, u32[]{:S(2)}) copy-start(s32[256]{0:T(256)} %get-tuple-element.33) | copy-start | bytes 3076
  55.8 13.1 %copy-start.8 = (s32[256]{0:T(256)S(1)}, s32[256]{0:T(256)}, u32[]{:S(2)}) copy-start(s32[256]{0:T(256)} %get-tuple-element.32) | copy-start | bytes 3076
  55.8 13.1 %copy-start.13 = (s32[256]{0:T(256)S(1)}, s32[256]{0:T(256)}, u32[]{:S(2)}) copy-start(s32[256]{0:T(256)} %iota_xor_fusion.1) | copy-start | bytes 3076
  58.3 11.0 %copy-start.10 = (s32[256]{0:T(256)S(1)}, s32[256]{0:T(256)}, u32[]{:S(2)}) copy-start(s32[256]{0:T(256)} %param.6) | copy-start | bytes 3076
  69.0 1.4 %copy-start.2 = (f32[256,256]{0,1:T(8,128)S(1)}, f32[256,256]{0,1:T(8,128)}, u32[]{:S(2)}) copy-start(f32[256,256]{0,1:T(8,128)} %get-tuple-element.2) | copy-start | bytes 786436
  69.0 1.4 %copy-start.3 = (f32[256,256]{0,1:T(8,128)S(1)}, f32[256,256]{0,1:T(8,128)}, u32[]{:S(2)}) copy-start(f32[256,256]{0,1:T(8,128)} %get-tuple-element.3) | copy-start | bytes 786436
  69.0 1.4 %copy-start.4 = (f32[256,256]{0,1:T(8,128)S(1)}, f32[256,256]{0,1:T(8,128)}, u32[]{:S(2)}) copy-start(f32[256,256]{0,1:T(8,128)} %get-tuple-element.4) | copy-start | bytes 786436
  70.4 0.7 copy-start.11
  70.4 0.7 copy-start.12
  70.8 0.9 copy-start.18

commit v7 on v6

--- a/solution.py
+++ b/solution.py
@@ -70,7 +70,7 @@
     first_cos = jnp.cos(first_phase) * norm_scale
     first_sin = jnp.sin(first_phase) * norm_scale
     first_both = jnp.concatenate([first_cos, -first_sin], axis=1)
-    part = jnp.einsum("rab,ap->rbp", folded, first_both, precision=highest)
+    part = jnp.einsum("rab,ap->rbp", folded, first_both, precision=lax.Precision.HIGH)
     part_real, part_imag = part[:, :, :128], part[:, :, 128:]
     low_ids = jnp.arange(low_split, dtype=jnp.int32)
     twist_phase = 2.0 * math.pi / W * (low_ids[:, None] * lane_ids[None, :]).astype(jnp.float32)
@@ -94,7 +94,7 @@
             jnp.concatenate([last_sin, last_cos], axis=1),
         ]
     )
-    spec = jnp.einsum("rbp,bq->rqp", turned, last_both, precision=highest)
+    spec = jnp.einsum("rbp,bq->rqp", turned, last_both, precision=lax.Precision.HIGH)
     spec_real, spec_imag = spec[:, :high_count], spec[:, high_count:]
     return (spec_real, spec_imag)
 
@@ -249,7 +249,7 @@
     step_grad = lax.dot_general(
         -step_size * stacked, tabs, (((0,), (0,)), ((), ())), precision=lax.Precision.HIGH
     )
-    updated = (coef_rows + step_grad).reshape(coefficients.shape)
+    updated = coefficients + step_grad.reshape(coefficients.shape)
     return (updated, misfit)
 
 

time: 98.4 us -> 97.1 us (0.987)
  matrix products: 16.8 us -> 15 us
  other arithmetic: 19.7 us -> 21.1 us
    dot_general x1, matrix products: 3.69 us -> 1.35 us  [step_body(): lax.dot_general(-step_size * stacked, tabs, (((0,), (0,)), ((), ())), pre...]
    add x0 -> x1, other arithmetic: none -> 1.19 us  [step_body(): updated = coefficients + step_grad.reshape(coefficients.shape)]
  transfers between devices with their start and end apart: 2 -> 2, of which waited for: 1 -> 1; matrix products, arithmetic and copies ran while one was open for 25% -> 26% of each run, Pallas kernels for 0% -> 0%
where the time goes in v7:
time: 97.1 us; the launch traced here: 96.6 us
  other arithmetic  21.1 us (22%)
  blocking collectives  18.8 us (19%)
  starting transfers between devices  17.6 us (18%)
  matrix products  15 us (15%)
  local copies, waits for them, and re-layouts  12.4 us (13%)
  waiting for transfers between devices  9.45 us (10%)
  between operations  2.36 us (2%)
    all_to_all x1, blocking collectives, step_body(): received = lax.all_to_all(payload, ANG_SL, 0, 0, tiled=True)  18.8 us
    all_to_all x1, starting transfers between devices, step_body(): received = lax.all_to_all(payload, ANG_SL, 0, 0, tiled=True)  9.85 us
    all_to_all x1, waiting for transfers between devices, step_body(): received = lax.all_to_all(payload, ANG_SL, 0, 0, tiled=True)  9.45 us
    ppermute x1, starting transfers between devices, from_behind(): return lax.ppermute(value, axis, pairs)  7.73 us
    mul x1, other arithmetic, step_body(): jnp.cos(phase_tab) * norm_scale  5.36 us
    dot_general x1, matrix products, step_body(): lax.dot_general(tabs, tabs, (((1,), (1,)), ((), ())), precision=highest)  5.31 us
    transpose x1, local copies, waits for them, and re-layouts, step_body(): payload = spectra.transpose(2, 3, 0, 1, 4).reshape(dev_count, -1)  4.01 us
    dot_general x1, matrix products, to_image(): lax.dot_general(tabs, coef, (((1,), (1,)), ((), ())), precision=highest)  3.29 us
  transfers between devices with their start and end apart: 2, of which 1 were waited for; matrix products, arithmetic and copies ran while one was open for 26% of the time, Pallas kernels for 0%

profile of v7, /device:TPU:1, one launch (start us, length us, event | category | flops | bytes accessed | tf_op | source)
XLA Modules:
  0.0 96.6 jit_solution(14919733971810676738)
XLA Ops:
  0.6 0.7 slice.94
  1.3 7.7 %collective-permute-start = (f32[2,4,256]{2,1,0:T(4,128)S(1)}, f32[2,4,256]{2,1,0:T(4,128)S(1)}, u32[]{:S(2)}, u32[]{:S(2)}) collective-permute-start(f32[2,4,256]{2,1,0:T(4,128)S(1)} %slice.94), channel_id=1, source_target_pairs={{0,128},{2,130},{4,132},{6,134},{8,136},{10,138},{12,140},{14,142}... | collective-permute-start | bytes 24584 | tf_op jit(solution)/shard_map/ppermute | solution.py:28
  9.1 0.8 multiply_negate_fusion
  9.8 0.8 fusion.81
  10.6 0.7 fusion.100
  11.3 0.7 fusion.104
  16.7 0.7 convert_element_type.78
  17.8 5.4 %fusion.3 = (f32[256,1280]{1,0:T(8,128)S(1)}, f32[256,1280]{1,0:T(8,128)S(1)}) fusion(f32[1280]{0:T(1024)S(1)} %add_convert_fusion, f32[256]{0:T(256)} %param.8), kind=kLoop, calls=%fused_computation.6 | loop fusion | flops 983040 | bytes 2627584 | tf_op jit(solution)/shard_map/mul | solution.py:169
  23.2 5.3 %fusion.1 = f32[512,512]{0,1:T(8,128)} fusion(f32[256,1280]{1,0:T(8,128)S(1)} %get-tuple-element.14, f32[256,1280]{1,0:T(8,128)S(1)} %get-tuple-element.13), kind=kOutput, calls=%fused_computation.4 | convolution fusion | flops 4027187200 | bytes 3670016 | tf_op jit(solution)/shard_map/dot_general | solution.py:196
  29.3 1.2 %fusion.57 = f32[8,64,256]{2,1,0:T(8,128)S(1)} fusion(f32[8,64,64]{2,1,0:T(8,128)S(1)} %reshape.334, f32[64,128]{1,0:T(8,128)} %get-tuple-element.26, f32[64,128]{1,0:T(8,128)} %get-tuple-element.27), kind=kOutput, calls=%fused_computation.84 | convolution fusion | flops 50348032 | bytes 720896 | tf_op jit(solution)/shard_map/rab,ap->rbp/dot_general | solution.py:73
  30.5 0.8 multiply_add_fusion
  31.7 1.0 %copy.16 = f32[8,32,128]{1,2,0:T(8,128)} copy(f32[8,32,128]{2,1,0:T(8,128)S(1)} %get-tuple-element.10) | data formatting | bytes 262144 | tf_op jit(solution)/shard_map/slice | solution.py:98
  32.7 1.0 %copy.17 = f32[8,32,128]{1,2,0:T(8,128)} copy(f32[8,32,128]{2,1,0:T(8,128)S(1)} %get-tuple-element.11) | data formatting | bytes 262144 | tf_op jit(solution)/shard_map/slice | solution.py:98
  33.7 2.3 %maximum_bitcast_fusion = f32[32,8,2,8,16]{0,4,1,3,2:T(8,128)} fusion(f32[1,8,32,8,16]{2,4,3,1,0:T(8,128)} %bitcast.51, f32[1,8,32,8,16]{2,4,3,1,0:T(8,128)} %bitcast.50), kind=kLoop, calls=%fused_computation.15 | loop fusion | flops 65536 | bytes 524288 | tf_op jit(solution)/shard_map/transpose | solution.py:127
  36.0 4.0 %copy.18 = f32[32,8,2,8,16]{4,3,2,1,0:T(8,128)} copy(f32[32,8,2,8,16]{0,4,1,3,2:T(8,128)} %maximum_bitcast_fusion) | data formatting | bytes 524288 | tf_op jit(solution)/shard_map/transpose | solution.py:127
  40.0 3.0 %all_to_all.19 = f32[256,1,256]{2,1,0:T(1,128)} reshape(f32[32,8,2,8,16]{4,3,2,1,0:T(8,128)} %copy.18) | data formatting | bytes 524288 | tf_op jit(solution)/shard_map/all_to_all | solution.py:128
  43.0 9.9 %all-to-all-start = ((f32[256,1,256]{2,1,0:T(1,128)}), f32[256,1,256]{2,1,0:T(1,128)S(1)}, u32[]{:S(2)}, u32[]{:S(2)}) async-start(f32[256,1,256]{2,1,0:T(1,128)} %all_to_all.19), calls=%async_computation | async-start | bytes 524288 | tf_op jit(solution)/shard_map/all_to_all | solution.py:128
  53.4 2.3 %fusion.148 = (f32[256,256]{0,1:T(8,128)}, f32[256,256]{0,1:T(8,128)}, f32[256,256]{0,1:T(8,128)}) fusion(f32[512,512]{0,1:T(8,128)} %fusion.1), kind=kLoop, calls=%fused_computation.235 | loop fusion | flops 196608 | bytes 1835008 | tf_op jit(solution)/shard_map/neg | solution.py:201
  55.6 3.3 %fusion.2 = f32[512,256]{0,1:T(8,128)} fusion(f32[256,1280]{1,0:T(8,128)S(1)} %bitcast.49, f32[256,1280]{1,0:T(8,128)S(1)} %get-tuple-element.14, f32[256,1280]{1,0:T(8,128)S(1)} %get-tuple-element.13), kind=kOutput, calls=%fused_computation.5 | convolution fusion | flops 2013921280 | bytes 4456448 | tf_op jit(solution)/shard_map/dot_general | solution.py:173
  58.9 9.4 %all-to-all-done = f32[256,1,256]{2,1,0:T(1,128)S(1)} async-done(((f32[256,1,256]{2,1,0:T(1,128)}), f32[256,1,256]{2,1,0:T(1,128)S(1)}, u32[]{:S(2)}, u32[]{:S(2)}) %all-to-all-start) | async-done | bytes 262176 | tf_op jit(solution)/shard_map/all_to_all | solution.py:128
  72.4 18.8 %all_to_all.22 = f32[256,1,10]{2,1,0:T(1,128)S(1)} all-to-all(f32[256,1,10]{2,1,0:T(1,128)S(1)} %copy.21), channel_id=1, replica_groups=mesh['ang_0'=8,'ang_1'=2,'ang_2'=4,'ang_3'=2,'sl'=2] {'ang_0','ang_1','a..., dimensions={0} | all-to-all | bytes 20480 | tf_op jit(solution)/shard_map/all_to_all | solution.py:245
  93.4 1.3 %fusion = f32[256,1280]{1,0:T(8,128)S(1)} fusion(f32[256,1280]{1,0:T(8,128)S(1)} %get-tuple-element.14, f32[256,1280]{1,0:T(8,128)S(1)} %get-tuple-element.13, f32[256,128]{0,1:T(8,128)S(1)} %get-tuple-element.12, f32[256,128]{0,1:T(8,128)S(1)} %get-tuple-element.20, f32[256,128]{0,1:T(8,128)S(1)} %get-tuple-element.19, f32[]{:T(128)} %bitcast.14), kind=kOutput, calls=%fused_computation.3 | convolution fusion | flops 1007812608 | bytes 4325380 | tf_op jit(solution)/shard_map/dot_general | solution.py:249
  94.7 1.2 %add.246 = f32[2,8,16,1280]{3,2,1,0:T(8,128)} add(f32[2,8,16,1280]{3,2,1,0:T(8,128)S(1)} %copy-done.1, f32[2,8,16,1280]{3,2,1,0:T(8,128)S(1)} %bitcast.48) | non-fusion elementwise | flops 327680 | bytes 3932160 | tf_op jit(solution)/shard_map/add | solution.py:252
  95.9 0.6 reshape.337
  (95 shorter events, 11.4 us)
Async XLA Ops:
  1.3 27.3 %collective-permute-start = (f32[2,4,256]{2,1,0:T(4,128)S(1)}, f32[2,4,256]{2,1,0:T(4,128)S(1)}, u32[]{:S(2)}, u32[]{:S(2)}) collective-permute-start(f32[2,4,256]{2,1,0:T(4,128)S(1)} %slice.94), channel_id=1, source_target_pairs={{0,128},{2,130},{4,132},{6,134},{8,136},{10,138},{12,140},{14,142}... | collective-permute-start | bytes 24584 | tf_op jit(solution)/shard_map/ppermute | solution.py:28
  23.2 5.3 %copy-start.11 = (s32[256]{0:T(256)S(1)}, s32[256]{0:T(256)}, u32[]{:S(2)}) copy-start(s32[256]{0:T(256)} %param.6) | copy-start | bytes 3076
  23.2 5.8 %copy-start.3 = (f32[2,4,4352]{2,1,0:T(4,128)S(1)}, f32[2,4,4352]{2,1,0:T(4,128)}, u32[]{:S(2)}) copy-start(f32[2,4,4352]{2,1,0:T(4,128)} %param.5) | copy-start | bytes 417796
  23.2 5.8 %slice-start = ((f32[2,4,4352]{2,1,0:T(4,128)}), f32[2,4,3840]{2,1,0:T(4,128)S(1)}, s32[]{:S(2)}) async-start(f32[2,4,4352]{2,1,0:T(4,128)} %param.5), calls=%async_computation.2 | async-start | bytes 245760 | tf_op jit(solution)/shard_map/slice | solution.py:55
  29.3 2.1 %copy-start.7 = (f32[64,32]{0,1:T(8,128)S(1)}, f32[64,32]{0,1:T(8,128)}, u32[]{:S(2)}) copy-start(f32[64,32]{0,1:T(8,128)} %get-tuple-element.31) | copy-start | bytes 24580
  29.3 2.1 %copy-start.8 = (f32[64,32]{0,1:T(8,128)S(1)}, f32[64,32]{0,1:T(8,128)}, u32[]{:S(2)}) copy-start(f32[64,32]{0,1:T(8,128)} %fusion.104) | copy-start | bytes 24580
  40.0 13.1 %copy-start.19 = (f32[16]{0:T(128)S(1)}, f32[16]{0:T(128)}, u32[]{:S(2)}) copy-start(f32[16]{0:T(128)} %get-tuple-element.25) | copy-start | bytes 196
  40.0 13.2 %copy-start.18 = (f32[16]{0:T(128)S(1)}, f32[16]{0:T(128)}, u32[]{:S(2)}) copy-start(f32[16]{0:T(128)} %get-tuple-element.24) | copy-start | bytes 196
  40.0 13.3 %copy-start.17 = (f32[16]{0:T(128)S(1)}, f32[16]{0:T(128)}, u32[]{:S(2)}) copy-start(f32[16]{0:T(128)} %get-tuple-element.22) | copy-start | bytes 196
  43.0 25.4 %all-to-all-start = ((f32[256,1,256]{2,1,0:T(1,128)}), f32[256,1,256]{2,1,0:T(1,128)S(1)}, u32[]{:S(2)}, u32[]{:S(2)}) async-start(f32[256,1,256]{2,1,0:T(1,128)} %all_to_all.19), calls=%async_computation | async-start | bytes 524288 | tf_op jit(solution)/shard_map/all_to_all | solution.py:128
  53.4 2.3 %copy-start = (f32[2,8,16,1280]{3,2,1,0:T(8,128)S(1)}, f32[2,8,16,1280]{3,2,1,0:T(8,128)}, u32[]{:S(2)}) copy-start(f32[2,8,16,1280]{3,2,1,0:T(8,128)} %param.9) | copy-start | bytes 3932164
  55.6 12.8 %copy-start.16 = (s32[256]{0:T(256)S(1)}, s32[256]{0:T(256)}, u32[]{:S(2)}) copy-start(s32[256]{0:T(256)} %iota_xor_fusion) | copy-start | bytes 3076
  55.6 13.1 %copy-start.9 = (s32[256]{0:T(256)S(1)}, s32[256]{0:T(256)}, u32[]{:S(2)}) copy-start(s32[256]{0:T(256)} %get-tuple-element.33) | copy-start | bytes 3076
  55.6 13.1 %copy-start.10 = (s32[256]{0:T(256)S(1)}, s32[256]{0:T(256)}, u32[]{:S(2)}) copy-start(s32[256]{0:T(256)} %get-tuple-element.32) | copy-start | bytes 3076
  55.6 13.1 %copy-start.15 = (s32[256]{0:T(256)S(1)}, s32[256]{0:T(256)}, u32[]{:S(2)}) copy-start(s32[256]{0:T(256)} %iota_xor_fusion.1) | copy-start | bytes 3076
  58.9 10.2 %copy-start.12 = (s32[256]{0:T(256)S(1)}, s32[256]{0:T(256)}, u32[]{:S(2)}) copy-start(s32[256]{0:T(256)} %param.6) | copy-start | bytes 3076
  68.4 1.1 %copy-start.2 = (f32[512,256]{0,1:T(8,128)S(1)}, f32[512,256]{0,1:T(8,128)}, u32[]{:S(2)}) copy-start(f32[512,256]{0,1:T(8,128)} %fusion.2) | copy-start | bytes 1572868
  68.8 1.4 %copy-start.4 = (f32[256,256]{0,1:T(8,128)S(1)}, f32[256,256]{0,1:T(8,128)}, u32[]{:S(2)}) copy-start(f32[256,256]{0,1:T(8,128)} %get-tuple-element.2) | copy-start | bytes 786436
  68.8 1.4 %copy-start.5 = (f32[256,256]{0,1:T(8,128)S(1)}, f32[256,256]{0,1:T(8,128)}, u32[]{:S(2)}) copy-start(f32[256,256]{0,1:T(8,128)} %get-tuple-element.3) | copy-start | bytes 786436
  68.8 1.4 %copy-start.6 = (f32[256,256]{0,1:T(8,128)S(1)}, f32[256,256]{0,1:T(8,128)}, u32[]{:S(2)}) copy-start(f32[256,256]{0,1:T(8,128)} %get-tuple-element.4) | copy-start | bytes 786436
  70.2 0.7 copy-start.13
  70.2 0.7 copy-start.14
  70.6 0.9 copy-start.20
  93.4 1.4 %copy-start.1 = (f32[2,8,16,1280]{3,2,1,0:T(8,128)S(1)}, f32[2,8,16,1280]{3,2,1,0:T(8,128)}, u32[]{:S(2)}) copy-start(f32[2,8,16,1280]{3,2,1,0:T(8,128)} %param.9) | copy-start | bytes 3932164
